TPU v7x, 256 devices: a whole 4x4x8 slice. The times are simulated.
256 devices in a mesh: space: 32 (over x, z), sub: 8 (over y, core).
Axes of the slice: x: 4, y: 4, z: 8, core: 2. Of those that a mesh axis runs over, the one named last changes fastest.
Arguments:
- offsets: float32 [32, 8, 32, 8, 4, 3, 128], P('space', 'sub'), may hold values from 0.5 to 7.5
- normals: float32 [32, 8, 32, 8, 4, 3, 128], P('space', 'sub'), may hold values from -6 to 6
- density: float32 [32, 8, 32, 8, 4, 128], P('space', 'sub'), may hold values from 0.3 to 3
- tile_brick: int32 [32, 8, 32, 8, 4], P('space', 'sub'), may hold values from 0 to 63
- tile_count: int32 [32, 8, 32, 8, 4], P('space', 'sub'), may hold values from 32 to 128, as said below
Outputs:
- indicator: float32 [512, 128, 128], P('space', 'sub')
- density_field: float32 [512, 128, 128], P('space', 'sub')
Inputs may be any that keep to these rules, and one draw needn't show every extreme that they name: `tile_count`: slots at and beyond a tile's count are padding; some tile holds 128 live points.
All inputs are finite; a program needn't handle non-finite values.
Results may differ from a plain program's by a relative error of at most 0.0003.
Values sent between devices are 32-bit elements; how exact they have to be, the bound alone decides.
No kernel may reach another device: no remote copies, remote signals or barrier semaphores. Data moves between devices by JAX's collectives and lax.ppermute only.
A program may use at most 192 MiB of HBM per device.

v0:
```python
import jax
import jax.numpy as jnp
from jax import lax
from jax.sharding import PartitionSpec as P

BRICK = 8
CX = 16
CY = 16
CZ = 128
LEVELS = 4
SWEEPS = 2
COARSE = 8

screen_weight = 0.05
relax_weight = 0.8

HALO0 = 4
HALO1 = 4


def exchange(x, width, dim_x, dim_y):
    for axis, dim in (("space", dim_x), ("sub", dim_y)):
        devices = lax.axis_size(axis)
        length = x.shape[dim]
        up = [(i, i + 1) for i in range(devices - 1)]
        down = [(j, i) for i, j in up]
        last = lax.slice_in_dim(x, length - width, length, axis=dim)
        first = lax.slice_in_dim(x, 0, width, axis=dim)
        before = lax.ppermute(last, axis, up)
        after = lax.ppermute(first, axis, down)
        x = jnp.concatenate([before, x, after], axis=dim)
    return x


def crop(x, h_from, h_to):
    d = h_from - h_to
    if d == 0:
        return x
    return x[d:-d, d:-d]


def inside_mask(nx, ny, nz, halo):
    dev_x = lax.axis_index("space")
    dev_y = lax.axis_index("sub")
    total_x = lax.axis_size("space") * nx
    total_y = lax.axis_size("sub") * ny
    gx = lax.broadcasted_iota(jnp.int32, (nx + 2 * halo, ny + 2 * halo, nz), 0) + dev_x * nx - halo
    gy = lax.broadcasted_iota(jnp.int32, (nx + 2 * halo, ny + 2 * halo, nz), 1) + dev_y * ny - halo
    ok = (gx >= 0) & (gx < total_x) & (gy >= 0) & (gy < total_y)
    return ok.astype(jnp.float32)


def operate_ext(u, screen_c, scale):
    c = u[1:-1, 1:-1, :]
    zp = jnp.pad(c, ((0, 0), (0, 0), (1, 1)))
    total = u[2:, 1:-1] + u[:-2, 1:-1]
    total = total + u[1:-1, 2:] + u[1:-1, :-2]
    total = total + zp[:, :, 2:] + zp[:, :, :-2]
    return (6.0 * c - total) * scale + screen_c * c


def sweep_ext(u, h, f, screen, diag, mask, scale):
    fc, sc, dc = crop(f, h, h - 1), crop(screen, h, h - 1), crop(diag, h, h - 1)
    new = crop(u, h, h - 1) + relax_weight * (fc - operate_ext(u, sc, scale)) / dc
    return new * crop(mask, h, h - 1)


def pair_matrix(n):
    rows = lax.broadcasted_iota(jnp.int32, (n, n // 2), 0) // 2
    cols = lax.broadcasted_iota(jnp.int32, (n, n // 2), 1)
    return (rows == cols).astype(jnp.float32)


def restrict(field):
    sx, sy, sz = field.shape
    zs = jnp.dot(
        field.reshape(sx * sy, sz), pair_matrix(sz), precision=lax.Precision.HIGHEST
    ).reshape(sx, sy, sz // 2)
    xs = zs.reshape(sx // 2, 2, sy, sz // 2).sum(axis=1)
    ys = xs.reshape(sx // 2, sy // 2, 2, sz // 2).sum(axis=2)
    return ys * 0.125


def prolong(field):
    sx, sy, sz = field.shape
    zs = jnp.dot(
        field.reshape(sx * sy, sz), pair_matrix(2 * sz).T, precision=lax.Precision.HIGHEST
    ).reshape(sx, sy, 2 * sz)
    return jnp.repeat(jnp.repeat(zs, 2, axis=0), 2, axis=1)


def neighbours(padded):
    total = padded[2:, 1:-1, 1:-1] + padded[:-2, 1:-1, 1:-1]
    total = total + padded[1:-1, 2:, 1:-1] + padded[1:-1, :-2, 1:-1]
    return total + padded[1:-1, 1:-1, 2:] + padded[1:-1, 1:-1, :-2]


def operate(field, screen, level_index):
    return (6.0 * field - neighbours(jnp.pad(field, 1))) * (0.25**level_index) + screen * field


def sweep(field, forcing, screen, diagonal, level_index):
    return field + relax_weight * (forcing - operate(field, screen, level_index)) / diagonal


def vcycle_global(forcing, level_index, screens):
    screen = screens[level_index]
    diagonal = 6.0 * (0.25**level_index) + screen
    field = relax_weight * forcing / diagonal
    if level_index == LEVELS - 1:
        for _ in range(COARSE - 1):
            field = sweep(field, forcing, screen, diagonal, level_index)
        return field
    for _ in range(SWEEPS - 1):
        field = sweep(field, forcing, screen, diagonal, level_index)
    residual = forcing - operate(field, screen, level_index)
    correction = vcycle_global(restrict(residual), level_index + 1, screens)
    field = field + prolong(correction)
    for _ in range(SWEEPS):
        field = sweep(field, forcing, screen, diagonal, level_index)
    return field


def splat(packed):
    tiles, _, slots = packed.shape
    centers = jnp.arange(BRICK, dtype=jnp.float32) + 0.5
    wx, wy, wz = [
        jnp.maximum(0.0, 1.0 - jnp.abs(packed[:, row, None, :] - centers[None, :, None]))
        for row in range(3)
    ]
    planar = (wx[:, :, None, :] * wy[:, None, :, :]).reshape(tiles, BRICK * BRICK, slots)
    loaded = (packed[:, 3:7, None, :] * wz[:, None, :, :]).reshape(tiles, 4 * BRICK, slots)
    partials = jnp.einsum("tbs,tas->tba", loaded, planar, precision=lax.Precision.HIGH)
    brick_total = CX // BRICK * (CY // BRICK) * (CZ // BRICK)
    brick_row = packed[:, 7, :brick_total]
    numbers = lax.broadcasted_iota(jnp.float32, (tiles, brick_total), 1)
    onehot = (brick_row == numbers).astype(jnp.float32)
    sums = jnp.einsum("tk,tba->kba", onehot, partials, precision=lax.Precision.HIGH)
    return sums


def gather_all(block, space_count, sub_count):
    channels, nx, ny, nz = block.shape
    devices = space_count * sub_count
    flat = block.reshape(1, -1, 128)
    sent = jnp.broadcast_to(flat, (devices,) + flat.shape[1:])
    every = lax.all_to_all(sent, ("space", "sub"), 0, 0, tiled=True)
    every = every.reshape(space_count, sub_count, channels, nx, ny, nz)
    every = every.transpose(2, 0, 3, 1, 4, 5)
    return every.reshape(channels, space_count * nx, sub_count * ny, nz)


def to_grid(sums):
    shaped = sums.reshape(CX // BRICK, CY // BRICK, CZ // BRICK, 4, BRICK, BRICK, BRICK)
    return shaped.transpose(3, 0, 5, 1, 6, 2, 4).reshape(4, CX, CY, CZ)


def on_device(offsets, normals, density, tile_brick, tile_count):
    space_count = lax.axis_size("space")
    sub_count = lax.axis_size("sub")
    devices = space_count * sub_count
    tiles_each = offsets.shape[4]
    slot_total = offsets.shape[6]

    slot_numbers = lax.broadcasted_iota(jnp.int32, (devices, tiles_each, 1, slot_total), 3)
    live = (slot_numbers < tile_count.reshape(devices, tiles_each, 1, 1)).astype(jnp.float32)
    samples = jnp.concatenate(
        [
            normals.reshape(devices, tiles_each, 3, slot_total),
            density.reshape(devices, tiles_each, 1, slot_total),
        ],
        axis=2,
    ) * live
    brick_row = jnp.broadcast_to(
        tile_brick.reshape(devices, tiles_each, 1, 1).astype(jnp.float32),
        (devices, tiles_each, 1, slot_total),
    )
    packed = jnp.concatenate(
        [offsets.reshape(devices, tiles_each, 3, slot_total), samples, brick_row], axis=2
    )
    received = lax.all_to_all(packed, ("space", "sub"), 0, 0, tiled=True)
    sums = splat(received.reshape(devices * tiles_each, 8, slot_total))
    grid = to_grid(sums)
    density_field = grid[3]

    h0 = HALO0
    g = exchange(grid, h0, 1, 2)
    vx, vy, vz, rho0 = g[0], g[1], g[2], g[3]
    mask0 = inside_mask(CX, CY, CZ, h0)
    hf = h0 - 1
    vzc = jnp.pad(crop(vz, h0, hf), ((0, 0), (0, 0), (1, 1)))
    change = vx[2:, 1:-1] - vx[:-2, 1:-1] + (vy[1:-1, 2:] - vy[1:-1, :-2])
    change = change + (vzc[:, :, 2:] - vzc[:, :, :-2])
    m0 = crop(mask0, h0, hf)
    f0 = -0.5 * change * m0
    screen0 = screen_weight * crop(rho0, h0, hf)
    diag0 = 6.0 + screen0
    u = relax_weight * f0 / diag0 * m0
    u = sweep_ext(u, hf, f0, screen0, diag0, m0, 1.0)
    hu0 = hf - 1
    residual0 = crop(f0, hf, 0) - operate_ext(
        crop(u, hu0, 1), crop(screen0, hf, 0), 1.0
    )

    h1 = HALO1
    f1 = restrict(residual0)
    rho1 = restrict(density_field)
    nx1, ny1, nz1 = f1.shape
    both = exchange(jnp.stack([f1, rho1]), h1, 1, 2)
    f1e, rho1e = both[0], both[1]
    mask1 = inside_mask(nx1, ny1, nz1, h1)
    scale1 = 0.25
    screen1 = screen_weight * rho1e
    diag1 = 6.0 * scale1 + screen1
    u1 = relax_weight * f1e / diag1 * mask1
    u1 = sweep_ext(u1, h1, f1e, screen1, diag1, mask1, scale1)
    hu1 = h1 - 1
    residual1 = crop(f1e, h1, 0) - operate_ext(crop(u1, hu1, 1), crop(screen1, h1, 0), scale1)

    f2 = restrict(residual1)
    nx2, ny2, nz2 = f2.shape

    rho2 = restrict(rho1)
    both2 = gather_all(jnp.stack([f2, rho2]), space_count, sub_count)
    f2g, rho2g = both2[0], both2[1]
    rho3g = restrict(rho2g)
    screens = [None, None, screen_weight * rho2g, screen_weight * rho3g]
    c2g = vcycle_global(f2g, 2, screens)
    hc2 = (hu1 + 1) // 2
    c2p = jnp.pad(c2g, ((hc2, hc2), (hc2, hc2), (0, 0)))
    c2 = lax.dynamic_slice(
        c2p,
        (lax.axis_index("space") * nx2, lax.axis_index("sub") * ny2, 0),
        (nx2 + 2 * hc2, ny2 + 2 * hc2, nz2),
    )

    u1 = u1 + crop(prolong(c2), 2 * hc2, hu1)
    hcur = hu1
    while hcur > 1:
        u1 = sweep_ext(
            u1,
            hcur,
            crop(f1e, h1, hcur),
            crop(screen1, h1, hcur),
            crop(diag1, h1, hcur),
            crop(mask1, h1, hcur),
            scale1,
        )
        hcur -= 1
    c1 = u1

    u = u + crop(prolong(c1), 2, hu0)
    hcur = hu0
    for _ in range(SWEEPS):
        u = sweep_ext(
            u,
            hcur,
            crop(f0, hf, hcur),
            crop(screen0, hf, hcur),
            crop(diag0, hf, hcur),
            crop(m0, hf, hcur),
            1.0,
        )
        hcur -= 1
    indicator = crop(u, hcur, 0)
    return (indicator, density_field)


def solution(mesh):
    placed = (
        P("space", "sub", None, None, None, None, None),
        P("space", "sub", None, None, None, None, None),
        P("space", "sub", None, None, None, None),
        P("space", "sub", None, None, None),
        P("space", "sub", None, None, None),
    )
    return jax.shard_map(
        on_device,
        mesh=mesh,
        in_specs=placed,
        out_specs=(P("space", "sub", None), P("space", "sub", None)),
        check_vma=False,
    )
```

profile of v0, /device:TPU:1, one launch (start us, length us, event | category | flops | bytes accessed | tf_op | source)
XLA Modules:
  0.0 350.6 jit_solution(6957076118978251946)
XLA Ops:
  0.6 0.7 convert_element_type.68
  1.5 2.0 copy.163
  4.0 2.0 copy.162
  6.0 1.1 maximum_multiply_fusion
  7.2 1.2 broadcast_in_dim.18
  8.5 3.4 pad_maximum_fusion
  11.8 17.3 %all-to-all-start = ((f32[256,4,8,128]{3,2,1,0:T(8,128)}), f32[256,4,8,128]{3,2,1,0:T(8,128)}, u32[]{:S(2)}, u32[]{:S(2)}) async-start(f32[256,4,8,128]{3,2,1,0:T(8,128)} %pad_maximum_fusion), calls=%async_computation | async-start | bytes 8388608 | tf_op jit(solution)/shard_map/all_to_all | solution.py:181
  29.3 0.8 fusion.183
  30.2 96.1 %all-to-all-done = f32[256,4,8,128]{3,2,1,0:T(8,128)} async-done(((f32[256,4,8,128]{3,2,1,0:T(8,128)}), f32[256,4,8,128]{3,2,1,0:T(8,128)}, u32[]{:S(2)}, u32[]{:S(2)}) %all-to-all-start) | async-done | bytes 4194336 | tf_op jit(solution)/shard_map/all_to_all | solution.py:181
  126.2 2.6 slice.777
  128.9 6.9 %fusion.302 = (f32[1024,1,128]{2,1,0:T(1,128)S(1)}, f32[1024,1,128]{2,1,0:T(1,128)}, f32[1024,1,128]{2,1,0:T(1,128)}) fusion(f32[1024,8,128]{2,1,0:T(8,128)} %bitcast.5), kind=kLoop, calls=%fused_computation.470 | loop fusion | bytes 3145728 | tf_op jit(solution)/shard_map/slice | solution.py:128
  135.8 2.6 slice.778
  138.4 0.7 fusion.60
  139.2 1.1 copy.168
  140.3 6.0 %subtract_maximum_fusion.2 = (f32[1024,8,128]{2,1,0:T(8,128)}, f32[1024,8,128]{2,1,0:T(8,128)}, f32[1024,8,128]{2,1,0:T(8,128)}) fusion(f32[8]{0:T(128)S(1)} %iota_add_fusion, f32[1024,128]{1,0:T(8,128)S(1)} %bitcast.145, f32[1024,128]{1,0:T(8,128)} %bitcast.147, f32[1024,128]{1,0:T(8,128)} %bitcast.146), kind=kLoop, calls=%fused_computation.14 | loop fusion | flops 12582912 | bytes 14155808 | tf_op jit(solution)/shard_map/max | solution.py:128
  146.3 31.0 %fusion.7 = f32[32,64,1024]{1,0,2:T(8,128)} fusion(f32[1024,8,128]{2,1,0:T(8,128)} %get-tuple-element.34, f32[1024,8,128]{2,1,0:T(8,128)} %get-tuple-element.33, f32[1024,8,128]{2,1,0:T(8,128)} %get-tuple-element.32, f32[1024,4,128]{2,1,0:T(4,128)S(1)} %slice.778), kind=kOutput, calls=%fused_computation.7 | convolution fusion | flops 1623195648 | bytes 23068672 | tf_op jit(solution)/shard_map/tbs,tas->tba/dot_general | solution.py:133
  177.3 13.0 %copy.169 = f32[32,64,1024]{2,1,0:T(8,128)} copy(f32[32,64,1024]{1,0,2:T(8,128)} %fusion.7) | data formatting | bytes 16777216 | tf_op jit(solution)/shard_map/tk,tba->kba/dot_general | solution.py:138
  190.3 8.3 %convolution_bitcast_fusion = f32[4,2,8,2,8,16,8]{5,4,2,6,0,3,1:T(8,128)} fusion(pred[2,2,16,1024,1,1,1]{3,2,6,5,4,1,0:T(8,128)(4,1)S(1)} %bitcast.159, f32[4,8,8,8,1024,1,1]{4,3,2,1,0,6,5:T(8,128)} %bitcast.137), kind=kOutput, calls=%fused_computation.40 | convolution fusion | flops 805306368 | bytes 8978432 | tf_op jit(solution)/shard_map/tk,tba->kba/dot_general | solution.py:138
  198.5 7.0 %copy.170 = f32[4,2,8,2,8,16,8]{6,5,4,3,2,1,0:T(8,128)} copy(f32[4,2,8,2,8,16,8]{5,4,2,6,0,3,1:T(8,128)} %convolution_bitcast_fusion) | data formatting | bytes 1048576 | tf_op jit(solution)/shard_map/transpose | solution.py:155
  205.6 6.4 %reshape.194 = f32[4,16,16,128]{3,2,1,0:T(8,128)S(1)} reshape(f32[4,2,8,2,8,16,8]{6,5,4,3,2,1,0:T(8,128)} %copy.170) | data formatting | bytes 1048576 | tf_op jit(solution)/shard_map/reshape | solution.py:155
  212.0 0.7 fusion.304
  212.7 1.9 collective-permute-start
  214.6 1.3 collective-permute-start.1
  216.6 1.0 dot_general.59
  218.0 0.9 constant_dynamic-update-slice_fusion.2
  219.0 1.7 collective-permute-done.1
  220.7 0.9 constant_dynamic-update-slice_fusion
  221.7 5.0 %collective-permute-start.3 = (f32[4,24,4,128]{3,2,1,0:T(4,128)S(1)}, f32[4,24,4,128]{3,2,1,0:T(4,128)S(1)}, u32[]{:S(2)}, u32[]{:S(2)}) collective-permute-start(f32[4,24,4,128]{3,2,1,0:T(4,128)S(1)} %get-tuple-element.15), channel_id=1, source_target_pairs={{1,0},{2,1},{3,2},{4,3},{5,4},{6,5},{7,6},{9,8},{10,9},{11,10},{12... | collective-permute-start | bytes 589832 | tf_op jit(solution)/shard_map/ppermute | solution.py:30
  226.6 3.1 collective-permute-start.2
  229.7 1.4 collective-permute-done.3
  231.1 1.2 collective-permute-done.2
  233.9 1.3 collective-permute-start.5
  235.2 4.0 %collective-permute-start.4 = (f32[2,4,8,64]{3,2,1,0:T(8,128)S(1)}, f32[2,4,8,64]{3,2,1,0:T(8,128)S(1)}, u32[]{:S(2)}, u32[]{:S(2)}) collective-permute-start(f32[2,4,8,64]{3,2,1,0:T(8,128)S(1)} %get-tuple-element.28), channel_id=1, source_target_pairs={{0,8},{8,16},{16,24},{24,32},{32,40},{40,48},{48,56},{56,64},{64,7... | collective-permute-start | bytes 49160 | tf_op jit(solution)/shard_map/ppermute | solution.py:29
  239.5 0.7 collective-permute-done.4
  240.3 1.9 collective-permute-start.7
  242.2 5.5 %collective-permute-start.6 = (f32[2,16,4,64]{3,2,1,0:T(4,128)S(1)}, f32[2,16,4,64]{3,2,1,0:T(4,128)S(1)}, u32[]{:S(2)}, u32[]{:S(2)}) collective-permute-start(f32[2,16,4,64]{3,2,1,0:T(4,128)S(1)} %get-tuple-element.26), channel_id=1, source_target_pairs={{0,1},{1,2},{2,3},{3,4},{4,5},{5,6},{6,7},{8,9},{9,10},{10,11},{11... | collective-permute-start | bytes 98312 | tf_op jit(solution)/shard_map/ppermute | solution.py:29
  248.4 0.7 collective-permute-done.6
  249.3 1.1 slice_multiply_fusion.4
  250.8 0.7 pad_maximum_fusion.5
  251.6 1.0 broadcast_in_dim.39
  252.7 15.5 %all-to-all-start.1 = ((f32[256,8,128]{2,1,0:T(8,128)}), f32[256,8,128]{2,1,0:T(8,128)}, u32[]{:S(2)}, u32[]{:S(2)}) async-start(f32[256,8,128]{2,1,0:T(8,128)} %broadcast_in_dim.39), calls=%async_computation.1 | async-start | bytes 2097152 | tf_op jit(solution)/shard_map/all_to_all | solution.py:147
  268.2 1.6 squeeze.33
  269.8 28.2 %all-to-all-done.1 = f32[256,8,128]{2,1,0:T(8,128)} async-done(((f32[256,8,128]{2,1,0:T(8,128)}), f32[256,8,128]{2,1,0:T(8,128)}, u32[]{:S(2)}, u32[]{:S(2)}) %all-to-all-start.1) | async-done | bytes 1048608 | tf_op jit(solution)/shard_map/all_to_all | solution.py:147
  298.0 4.3 %reshape.199 = f32[32,8,2,4,4,32]{5,4,3,2,1,0:T(4,128)} reshape(f32[256,8,128]{2,1,0:T(8,128)} %all-to-all-done.1) | data formatting | bytes 2097152 | tf_op jit(solution)/shard_map/reshape | solution.py:148
  302.3 4.6 %copy.204 = f32[32,8,2,4,4,32]{5,1,4,3,0,2:T(8,128)S(1)} copy(f32[32,8,2,4,4,32]{5,4,3,2,1,0:T(4,128)} %reshape.199) | data formatting | bytes 2097152 | tf_op jit(solution)/shard_map/reshape | solution.py:148
  306.9 1.9 fusion.301
  309.5 0.7 copy.180
  310.7 2.4 fusion.25
  313.1 2.4 fusion.34
  315.5 5.0 %convolution_reduce_fusion.1 = f32[64,32,16]{1,2,0:T(8,128)} fusion(f32[64,2,32,32]{3,2,1,0:T(8,128)S(1)} %bitcast.142, s32[32]{0:T(128)S(1)} %get-tuple-element.43, s32[32]{0:T(128)S(1)} %get-tuple-element.44, pred[32]{0:T(512)(128)(4,1)S(1)} %compare_and_fusion), kind=kOutput, calls=%fused_computation.89 | convolution fusion | flops 25199616 | bytes 655648 | tf_op jit(solution)/shard_map/dot_general | solution.py:76
  320.5 2.0 copy.181
  322.5 1.0 bitcast_reduce_fusion.1
  323.4 2.2 copy.182
  325.7 5.0 %convolution_reduce_fusion = f32[64,32,16]{1,2,0:T(8,128)} fusion(f32[64,2,32,32]{3,2,1,0:T(8,128)S(1)} %bitcast.141, s32[32]{0:T(128)S(1)} %get-tuple-element.43, s32[32]{0:T(128)S(1)} %get-tuple-element.44, pred[32]{0:T(512)(128)(4,1)S(1)} %compare_and_fusion), kind=kOutput, calls=%fused_computation.88 | convolution fusion | flops 25199616 | bytes 655648 | tf_op jit(solution)/shard_map/dot_general | solution.py:76
  330.7 2.0 copy.183
  332.7 1.0 bitcast_reduce_fusion
  334.9 1.1 fusion.184
  336.0 2.0 copy.184
  338.0 1.3 broadcast_in_dim.40
  339.3 1.2 broadcast_in_dim.41
  341.0 1.1 copy-done.1
  342.1 2.3 fusion.46
  344.5 2.4 fusion.58
  349.3 0.8 fusion.97
  (153 shorter events, 9.9 us)
Async XLA Ops:
  0.6 2.9 copy-start.16
  3.7 2.4 copy-start.15
  11.8 114.4 %all-to-all-start = ((f32[256,4,8,128]{3,2,1,0:T(8,128)}), f32[256,4,8,128]{3,2,1,0:T(8,128)}, u32[]{:S(2)}, u32[]{:S(2)}) async-start(f32[256,4,8,128]{3,2,1,0:T(8,128)} %pad_maximum_fusion), calls=%async_computation | async-start | bytes 8388608 | tf_op jit(solution)/shard_map/all_to_all | solution.py:181
  29.2 204.4 %copy-start.26 = (pred[128]{0:T(512)(128)(4,1)}, pred[128]{0:T(512)(128)(4,1)S(1)}, u32[]{:S(2)}) copy-start(pred[128]{0:T(512)(128)(4,1)S(1)} %compare_and_fusion.2) | copy-start | bytes 388
  29.2 204.4 %copy-start.28 = (s32[128]{0:T(128)}, s32[128]{0:T(128)S(1)}, u32[]{:S(2)}) copy-start(s32[128]{0:T(128)S(1)} %get-tuple-element.39) | copy-start | bytes 1540
  29.2 204.4 %copy-start.30 = (s32[128]{0:T(128)}, s32[128]{0:T(128)S(1)}, u32[]{:S(2)}) copy-start(s32[128]{0:T(128)S(1)} %get-tuple-element.40) | copy-start | bytes 1540
  29.3 210.0 %copy-start.17 = (s32[64]{0:T(128)}, s32[64]{0:T(128)S(1)}, u32[]{:S(2)}) copy-start(s32[64]{0:T(128)S(1)} %get-tuple-element.41) | copy-start | bytes 772
  29.3 210.0 %copy-start.20 = (s32[64]{0:T(128)}, s32[64]{0:T(128)S(1)}, u32[]{:S(2)}) copy-start(s32[64]{0:T(128)S(1)} %get-tuple-element.42) | copy-start | bytes 772
  212.0 2.7 copy-start.4
  212.0 4.0 %slice-start = ((f32[4,2,8,2,8,16,8]{5,4,2,6,0,3,1:T(8,128)}), f32[1,2,8,2,8,16,8]{5,4,2,6,0,3,1:T(8,128)S(1)}, s32[]{:S(2)}) async-start(f32[4,2,8,2,8,16,8]{5,4,2,6,0,3,1:T(8,128)} %convolution_bitcast_fusion), calls=%async_computation.2 | async-start | bytes 2097152 | tf_op jit(solution)/shard_map/slice | solution.py:184
  212.7 5.3 %collective-permute-start = (f32[4,4,16,128]{3,2,1,0:T(8,128)}, f32[4,4,16,128]{3,2,1,0:T(8,128)}, u32[]{:S(2)}, u32[]{:S(2)}) collective-permute-start(f32[4,4,16,128]{3,2,1,0:T(8,128)} %get-tuple-element.17), channel_id=1, source_target_pairs={{0,8},{8,16},{16,24},{24,32},{32,40},{40,48},{48,56},{56,64},{64,7... | collective-permute-start | bytes 393224 | tf_op jit(solution)/shard_map/ppermute | solution.py:29
  214.6 24.6 %copy-start.23 = (pred[64]{0:T(512)(128)(4,1)}, pred[64]{0:T(512)(128)(4,1)S(1)}, u32[]{:S(2)}) copy-start(pred[64]{0:T(512)(128)(4,1)S(1)} %compare_and_fusion.1) | copy-start | bytes 196
  214.6 6.0 %collective-permute-start.1 = (f32[4,4,16,128]{3,2,1,0:T(8,128)}, f32[4,4,16,128]{3,2,1,0:T(8,128)}, u32[]{:S(2)}, u32[]{:S(2)}) collective-permute-start(f32[4,4,16,128]{3,2,1,0:T(8,128)} %get-tuple-element.16), channel_id=1, source_target_pairs={{8,0},{16,8},{24,16},{32,24},{40,32},{48,40},{56,48},{64,56},{72,6... | collective-permute-start | bytes 393224 | tf_op jit(solution)/shard_map/ppermute | solution.py:30
  216.6 2.3 copy-start.5
  221.7 9.4 %collective-permute-start.3 = (f32[4,24,4,128]{3,2,1,0:T(4,128)S(1)}, f32[4,24,4,128]{3,2,1,0:T(4,128)S(1)}, u32[]{:S(2)}, u32[]{:S(2)}) collective-permute-start(f32[4,24,4,128]{3,2,1,0:T(4,128)S(1)} %get-tuple-element.15), channel_id=1, source_target_pairs={{1,0},{2,1},{3,2},{4,3},{5,4},{6,5},{7,6},{9,8},{10,9},{11,10},{12... | collective-permute-start | bytes 589832 | tf_op jit(solution)/shard_map/ppermute | solution.py:30
  226.6 5.7 %collective-permute-start.2 = (f32[4,24,4,128]{3,2,1,0:T(4,128)S(1)}, f32[4,24,4,128]{3,2,1,0:T(4,128)S(1)}, u32[]{:S(2)}, u32[]{:S(2)}) collective-permute-start(f32[4,24,4,128]{3,2,1,0:T(4,128)S(1)} %get-tuple-element.14), channel_id=1, source_target_pairs={{0,1},{1,2},{2,3},{3,4},{4,5},{5,6},{6,7},{8,9},{9,10},{10,11},{11... | collective-permute-start | bytes 589832 | tf_op jit(solution)/shard_map/ppermute | solution.py:29
  232.9 0.7 copy-start.6
  233.9 5.6 %collective-permute-start.5 = (f32[2,4,8,64]{3,2,1,0:T(8,128)S(1)}, f32[2,4,8,64]{3,2,1,0:T(8,128)S(1)}, u32[]{:S(2)}, u32[]{:S(2)}) collective-permute-start(f32[2,4,8,64]{3,2,1,0:T(8,128)S(1)} %get-tuple-element.29), channel_id=1, source_target_pairs={{8,0},{16,8},{24,16},{32,24},{40,32},{48,40},{56,48},{64,56},{72,6... | collective-permute-start | bytes 49160 | tf_op jit(solution)/shard_map/ppermute | solution.py:30
  235.2 5.0 %collective-permute-start.4 = (f32[2,4,8,64]{3,2,1,0:T(8,128)S(1)}, f32[2,4,8,64]{3,2,1,0:T(8,128)S(1)}, u32[]{:S(2)}, u32[]{:S(2)}) collective-permute-start(f32[2,4,8,64]{3,2,1,0:T(8,128)S(1)} %get-tuple-element.28), channel_id=1, source_target_pairs={{0,8},{8,16},{16,24},{24,32},{32,40},{40,48},{48,56},{56,64},{64,7... | collective-permute-start | bytes 49160 | tf_op jit(solution)/shard_map/ppermute | solution.py:29
  239.5 11.1 %copy-start.18 = (s32[64]{0:T(128)S(1)}, s32[64]{0:T(128)}, u32[]{:S(2)}) copy-start(s32[64]{0:T(128)} %copy-done.17) | copy-start | bytes 772
  239.5 11.1 %copy-start.21 = (s32[64]{0:T(128)S(1)}, s32[64]{0:T(128)}, u32[]{:S(2)}) copy-start(s32[64]{0:T(128)} %copy-done.20) | copy-start | bytes 772
  239.5 11.1 %copy-start.24 = (pred[64]{0:T(512)(128)(4,1)S(1)}, pred[64]{0:T(512)(128)(4,1)}, u32[]{:S(2)}) copy-start(pred[64]{0:T(512)(128)(4,1)} %copy-done.23) | copy-start | bytes 196
  240.3 8.1 %collective-permute-start.7 = (f32[2,16,4,64]{3,2,1,0:T(4,128)S(1)}, f32[2,16,4,64]{3,2,1,0:T(4,128)S(1)}, u32[]{:S(2)}, u32[]{:S(2)}) collective-permute-start(f32[2,16,4,64]{3,2,1,0:T(4,128)S(1)} %get-tuple-element.27), channel_id=1, source_target_pairs={{1,0},{2,1},{3,2},{4,3},{5,4},{6,5},{7,6},{9,8},{10,9},{11,10},{12... | collective-permute-start | bytes 98312 | tf_op jit(solution)/shard_map/ppermute | solution.py:30
  242.2 6.8 %collective-permute-start.6 = (f32[2,16,4,64]{3,2,1,0:T(4,128)S(1)}, f32[2,16,4,64]{3,2,1,0:T(4,128)S(1)}, u32[]{:S(2)}, u32[]{:S(2)}) collective-permute-start(f32[2,16,4,64]{3,2,1,0:T(4,128)S(1)} %get-tuple-element.26), channel_id=1, source_target_pairs={{0,1},{1,2},{2,3},{3,4},{4,5},{5,6},{6,7},{8,9},{9,10},{10,11},{11... | collective-permute-start | bytes 98312 | tf_op jit(solution)/shard_map/ppermute | solution.py:29
  249.2 1.4 copy-start.12
  249.3 1.2 copy-start.10
  249.3 3.4 copy-start.8
  252.7 45.3 %all-to-all-start.1 = ((f32[256,8,128]{2,1,0:T(8,128)}), f32[256,8,128]{2,1,0:T(8,128)}, u32[]{:S(2)}, u32[]{:S(2)}) async-start(f32[256,8,128]{2,1,0:T(8,128)} %broadcast_in_dim.39), calls=%async_computation.1 | async-start | bytes 2097152 | tf_op jit(solution)/shard_map/all_to_all | solution.py:147
  268.1 57.6 %copy-start.32 = (pred[32]{0:T(512)(128)(4,1)}, pred[32]{0:T(512)(128)(4,1)S(1)}, u32[]{:S(2)}) copy-start(pred[32]{0:T(512)(128)(4,1)S(1)} %compare_and_fusion) | copy-start | bytes 100
  268.2 57.5 %copy-start.34 = (s32[32]{0:T(128)}, s32[32]{0:T(128)S(1)}, u32[]{:S(2)}) copy-start(s32[32]{0:T(128)S(1)} %get-tuple-element.43) | copy-start | bytes 388
  268.2 57.5 %copy-start.36 = (s32[32]{0:T(128)}, s32[32]{0:T(128)S(1)}, u32[]{:S(2)}) copy-start(s32[32]{0:T(128)S(1)} %get-tuple-element.44) | copy-start | bytes 388
  310.2 2.9 copy-start
  313.1 2.4 copy-start.2
  332.7 2.1 copy-start.33
  332.7 2.1 copy-start.35
  332.7 2.1 copy-start.37
  338.0 2.5 copy-start.3
  340.5 1.6 copy-start.1
  344.5 2.4 copy-start.19
  344.5 2.4 copy-start.22
  344.5 2.4 copy-start.25
  346.9 0.9 copy-start.9
  346.9 1.0 copy-start.11
  346.9 1.0 copy-start.13
  346.9 1.1 copy-start.14
  346.9 1.2 copy-start.27
  346.9 1.2 copy-start.29
  347.0 1.2 copy-start.31
  348.0 1.0 copy-start.7
where the time goes:
time: 356 us; the launch traced here: 351 us
  waiting for transfers between devices  130 us (37%)
  local copies, waits for them, and re-layouts  76.1 us (21%)
  starting transfers between devices  56.7 us (16%)
  matrix products  51.5 us (14%)
  other arithmetic  34 us (10%)
    all_to_all x1, waiting for transfers between devices, on_device(): received = lax.all_to_all(packed, ('space', 'sub'), 0, 0, tiled=True)  96.1 us
    dot_general x1, matrix products, splat(): jnp.einsum('tbs,tas->tba', loaded, planar, precision=lax.Precision.HIGH)  31 us
    all_to_all x1, waiting for transfers between devices, gather_all(): every = lax.all_to_all(sent, ('space', 'sub'), 0, 0, tiled=True)  28.2 us
    all_to_all x1, starting transfers between devices, on_device(): received = lax.all_to_all(packed, ('space', 'sub'), 0, 0, tiled=True)  17.3 us
    all_to_all x1, starting transfers between devices, gather_all(): every = lax.all_to_all(sent, ('space', 'sub'), 0, 0, tiled=True)  15.5 us
    ppermute x4, starting transfers between devices, exchange(): before = lax.ppermute(last, axis, up)  14.5 us
    dot_general x2, local copies, waits for them, and re-layouts, splat(): jnp.einsum('tk,tba->kba', onehot, partials, precision=lax.Precision.HIGH)  14.1 us
    dot_general x6, matrix products, restrict(): jnp.dot(field.reshape(sx * sy, sz), pair_matrix(sz), precision=lax.Precis...  10.7 us
  transfers between devices with their start and end apart: 10, of which 7 were waited for; matrix products, arithmetic and copies ran while one was open for 2% of the time, Pallas kernels for 0%

commit v1 on v0

--- a/solution.py
+++ b/solution.py
@@ -119,6 +119,74 @@
     for _ in range(SWEEPS):
         field = sweep(field, forcing, screen, diagonal, level_index)
     return field
+
+
+def lane_pairs(ny, nz):
+    rows = lax.broadcasted_iota(jnp.int32, (ny * nz, ny * nz // 4), 0)
+    cols = lax.broadcasted_iota(jnp.int32, (ny * nz, ny * nz // 4), 1)
+    coarse = (rows // nz // 2) * (nz // 2) + (rows % nz) // 2
+    return (coarse == cols).astype(jnp.float32)
+
+
+def restrict2d(field, ny, nz):
+    sx, lanes = field.shape
+    xs = field.reshape(sx // 2, 2, lanes).sum(axis=1)
+    ys = jnp.dot(xs, lane_pairs(ny, nz), precision=lax.Precision.HIGHEST)
+    return ys * 0.125
+
+
+def prolong2d(field, ny, nz):
+    spread = jnp.dot(field, lane_pairs(ny, nz).T, precision=lax.Precision.HIGHEST)
+    return jnp.repeat(spread, 2, axis=0)
+
+
+def operate2d(u, screen, scale, nz):
+    sx, lanes = u.shape
+    zi = lax.broadcasted_iota(jnp.int32, (sx, lanes), 1) % nz
+    xp = jnp.pad(u, ((0, 1), (0, 0)))[1:]
+    xm = jnp.pad(u, ((1, 0), (0, 0)))[:-1]
+    yp = jnp.pad(u, ((0, 0), (0, nz)))[:, nz:]
+    ym = jnp.pad(u, ((0, 0), (nz, 0)))[:, :-nz]
+    zp = jnp.where(zi < nz - 1, jnp.pad(u, ((0, 0), (0, 1)))[:, 1:], 0.0)
+    zm = jnp.where(zi > 0, jnp.pad(u, ((0, 0), (1, 0)))[:, :-1], 0.0)
+    total = xp + xm
+    total = total + yp + ym
+    total = total + zp + zm
+    return (6.0 * u - total) * scale + screen * u
+
+
+def vcycle2d(forcing, level_index, screens, shapes):
+    ny, nz = shapes[level_index]
+    screen = screens[level_index]
+    scale = 0.25**level_index
+    diagonal = 6.0 * scale + screen
+    field = relax_weight * forcing / diagonal
+
+    def sweep2d(u):
+        return u + relax_weight * (forcing - operate2d(u, screen, scale, nz)) / diagonal
+
+    if level_index == LEVELS - 1:
+        for _ in range(COARSE - 1):
+            field = sweep2d(field)
+        return field
+    for _ in range(SWEEPS - 1):
+        field = sweep2d(field)
+    residual = forcing - operate2d(field, screen, scale, nz)
+    correction = vcycle2d(restrict2d(residual, ny, nz), level_index + 1, screens, shapes)
+    field = field + prolong2d(correction, ny, nz)
+    for _ in range(SWEEPS):
+        field = sweep2d(field)
+    return field
+
+
+def coarse_solve(f2g, rho2g):
+    sx, ny, nz = f2g.shape
+    f = f2g.reshape(sx, ny * nz)
+    rho2 = rho2g.reshape(sx, ny * nz)
+    rho3 = restrict2d(rho2, ny, nz)
+    screens = [None, None, screen_weight * rho2, screen_weight * rho3]
+    shapes = [None, None, (ny, nz), (ny // 2, nz // 2)]
+    return vcycle2d(f, 2, screens, shapes).reshape(sx, ny, nz)
 
 
 def splat(packed):
@@ -223,9 +291,7 @@
     rho2 = restrict(rho1)
     both2 = gather_all(jnp.stack([f2, rho2]), space_count, sub_count)
     f2g, rho2g = both2[0], both2[1]
-    rho3g = restrict(rho2g)
-    screens = [None, None, screen_weight * rho2g, screen_weight * rho3g]
-    c2g = vcycle_global(f2g, 2, screens)
+    c2g = coarse_solve(f2g, rho2g)
     hc2 = (hu1 + 1) // 2
     c2p = jnp.pad(c2g, ((hc2, hc2), (hc2, hc2), (0, 0)))
     c2 = lax.dynamic_slice(

time: 356 us -> 349 us (0.980)
  other arithmetic: 34 us -> 26.8 us
  local copies, waits for them, and re-layouts: 76.1 us -> 82.8 us
  matrix products: 51.5 us -> 46.1 us
    dot_general x6 -> x4, matrix products: 10.7 us -> 0.72 us  [restrict(): jnp.dot(field.reshape(sx * sy, sz), pair_matrix(sz), precision=lax.Precis...]
    another operation x0 -> x2, local copies, waits for them, and re-layouts: none -> 6.66 us  [the longest x1 3.36 us: coarse_solve(): f = f2g.reshape(sx, ny * nz)]
    mul x1 -> x2, local copies, waits for them, and re-layouts: 0.7 us -> 6.96 us  [coarse_solve(): screens = [None, None, screen_weight * rho2, screen_weight * rho3]]
    add x10, other arithmetic: 8.61 us -> 2.78 us  [the longest x9 2.72 us: sweep2d(): u + relax_weight * (forcing - operate2d(u, screen, scale, nz)) / diagonal]
    dot_general x0 -> x3, matrix products: none -> 4.7 us  [the longest x2 3.24 us: restrict2d(): ys = jnp.dot(xs, lane_pairs(ny, nz), precision=lax.Precision.HIGHEST)]
    reduce_sum x2 -> x0, local copies, waits for them, and re-layouts: 4.02 us -> none  [restrict(): xs = zs.reshape(sx // 2, 2, sy, sz // 2).sum(axis=1)]
    unnamed x80 -> x40, local copies, waits for them, and re-layouts: 7.24 us -> 6.07 us
where the time goes in v1:
time: 349 us; the launch traced here: 344 us
  waiting for transfers between devices  130 us (37%)
  local copies, waits for them, and re-layouts  82.8 us (24%)
  starting transfers between devices  55.7 us (16%)
  matrix products  46.1 us (13%)
  other arithmetic  26.8 us (8%)
    all_to_all x1, waiting for transfers between devices, on_device(): received = lax.all_to_all(packed, ('space', 'sub'), 0, 0, tiled=True)  96.1 us
    dot_general x1, matrix products, splat(): jnp.einsum('tbs,tas->tba', loaded, planar, precision=lax.Precision.HIGH)  31 us
    all_to_all x1, waiting for transfers between devices, gather_all(): every = lax.all_to_all(sent, ('space', 'sub'), 0, 0, tiled=True)  28.6 us
    all_to_all x1, starting transfers between devices, on_device(): received = lax.all_to_all(packed, ('space', 'sub'), 0, 0, tiled=True)  17.3 us
    ppermute x4, starting transfers between devices, exchange(): before = lax.ppermute(last, axis, up)  14.5 us
    all_to_all x1, starting transfers between devices, gather_all(): every = lax.all_to_all(sent, ('space', 'sub'), 0, 0, tiled=True)  14.4 us
    dot_general x2, local copies, waits for them, and re-layouts, splat(): jnp.einsum('tk,tba->kba', onehot, partials, precision=lax.Precision.HIGH)  14.1 us
    ppermute x4, starting transfers between devices, exchange(): after = lax.ppermute(first, axis, down)  9.45 us
  transfers between devices with their start and end apart: 10, of which 7 were waited for; matrix products, arithmetic and copies ran while one was open for 2% of the time, Pallas kernels for 0%

profile of v1, /device:TPU:1, one launch (start us, length us, event | category | flops | bytes accessed | tf_op | source)
XLA Modules:
  0.0 343.5 jit_solution(10157164625813103457)
XLA Ops:
  0.6 0.8 convert_element_type.133
  1.6 2.0 copy.101
  3.6 0.9 copy.127
  4.8 2.0 copy.100
  6.8 1.1 maximum_multiply_fusion
  7.9 1.2 broadcast_in_dim.62
  9.2 3.4 pad_maximum_fusion
  12.5 17.3 %all-to-all-start = ((f32[256,4,8,128]{3,2,1,0:T(8,128)}), f32[256,4,8,128]{3,2,1,0:T(8,128)}, u32[]{:S(2)}, u32[]{:S(2)}) async-start(f32[256,4,8,128]{3,2,1,0:T(8,128)} %pad_maximum_fusion), calls=%async_computation | async-start | bytes 8388608 | tf_op jit(solution)/shard_map/all_to_all | solution.py:249
  30.0 0.8 fusion.120
  30.9 96.1 %all-to-all-done = f32[256,4,8,128]{3,2,1,0:T(8,128)} async-done(((f32[256,4,8,128]{3,2,1,0:T(8,128)}), f32[256,4,8,128]{3,2,1,0:T(8,128)}, u32[]{:S(2)}, u32[]{:S(2)}) %all-to-all-start) | async-done | bytes 4194336 | tf_op jit(solution)/shard_map/all_to_all | solution.py:249
  127.0 2.6 slice.777
  129.6 6.8 %fusion.343 = (f32[1024,1,128]{2,1,0:T(1,128)S(1)}, f32[1024,1,128]{2,1,0:T(1,128)}, f32[1024,1,128]{2,1,0:T(1,128)}) fusion(f32[1024,8,128]{2,1,0:T(8,128)} %bitcast.5), kind=kLoop, calls=%fused_computation.524 | loop fusion | bytes 3145728 | tf_op jit(solution)/shard_map/slice | solution.py:196
  136.4 2.6 slice.778
  139.1 0.7 fusion.81
  139.8 1.1 copy.106
  140.9 6.0 %subtract_maximum_fusion.2 = (f32[1024,8,128]{2,1,0:T(8,128)}, f32[1024,8,128]{2,1,0:T(8,128)}, f32[1024,8,128]{2,1,0:T(8,128)}) fusion(f32[8]{0:T(128)S(1)} %iota_add_fusion, f32[1024,128]{1,0:T(8,128)S(1)} %bitcast.114, f32[1024,128]{1,0:T(8,128)} %bitcast.116, f32[1024,128]{1,0:T(8,128)} %bitcast.115), kind=kLoop, calls=%fused_computation.14 | loop fusion | flops 12582912 | bytes 14155808 | tf_op jit(solution)/shard_map/max | solution.py:196
  146.9 31.0 %fusion.7 = f32[32,64,1024]{1,0,2:T(8,128)} fusion(f32[1024,8,128]{2,1,0:T(8,128)} %get-tuple-element.34, f32[1024,8,128]{2,1,0:T(8,128)} %get-tuple-element.33, f32[1024,8,128]{2,1,0:T(8,128)} %get-tuple-element.32, f32[1024,4,128]{2,1,0:T(4,128)S(1)} %slice.778), kind=kOutput, calls=%fused_computation.7 | convolution fusion | flops 1623195648 | bytes 23068672 | tf_op jit(solution)/shard_map/tbs,tas->tba/dot_general | solution.py:201
  177.9 13.0 %copy.107 = f32[32,64,1024]{2,1,0:T(8,128)} copy(f32[32,64,1024]{1,0,2:T(8,128)} %fusion.7) | data formatting | bytes 16777216 | tf_op jit(solution)/shard_map/tk,tba->kba/dot_general | solution.py:206
  190.8 8.2 %convolution_bitcast_fusion = f32[4,2,8,2,8,16,8]{5,4,2,6,0,3,1:T(8,128)} fusion(pred[2,2,16,1024,1,1,1]{3,2,6,5,4,1,0:T(8,128)(4,1)S(1)} %bitcast.128, f32[4,8,8,8,1024,1,1]{4,3,2,1,0,6,5:T(8,128)} %bitcast.109), kind=kOutput, calls=%fused_computation.24 | convolution fusion | flops 805306368 | bytes 8978432 | tf_op jit(solution)/shard_map/tk,tba->kba/dot_general | solution.py:206
  199.0 7.0 %copy.108 = f32[4,2,8,2,8,16,8]{6,5,4,3,2,1,0:T(8,128)} copy(f32[4,2,8,2,8,16,8]{5,4,2,6,0,3,1:T(8,128)} %convolution_bitcast_fusion) | data formatting | bytes 1048576 | tf_op jit(solution)/shard_map/transpose | solution.py:223
  206.1 6.5 %reshape.182 = f32[4,16,16,128]{3,2,1,0:T(8,128)S(1)} reshape(f32[4,2,8,2,8,16,8]{6,5,4,3,2,1,0:T(8,128)} %copy.108) | data formatting | bytes 1048576 | tf_op jit(solution)/shard_map/reshape | solution.py:223
  212.6 0.8 fusion.345
  213.3 1.9 collective-permute-start
  215.3 1.3 collective-permute-start.1
  216.6 0.7 copy.111
  217.2 1.0 dot_general.55
  218.6 0.9 constant_dynamic-update-slice_fusion.2
  219.5 1.1 constant_dynamic-update-slice_fusion.1
  220.6 0.7 collective-permute-done.1
  221.3 0.9 constant_dynamic-update-slice_fusion
  222.3 5.0 %collective-permute-start.3 = (f32[4,24,4,128]{3,2,1,0:T(4,128)S(1)}, f32[4,24,4,128]{3,2,1,0:T(4,128)S(1)}, u32[]{:S(2)}, u32[]{:S(2)}) collective-permute-start(f32[4,24,4,128]{3,2,1,0:T(4,128)S(1)} %get-tuple-element.15), channel_id=1, source_target_pairs={{1,0},{2,1},{3,2},{4,3},{5,4},{6,5},{7,6},{9,8},{10,9},{11,10},{12... | collective-permute-start | bytes 589832 | tf_op jit(solution)/shard_map/ppermute | solution.py:30
  227.3 3.1 collective-permute-start.2
  230.3 1.4 collective-permute-done.3
  231.7 1.2 collective-permute-done.2
  233.6 1.5 fusion.95
  235.6 1.3 collective-permute-start.5
  236.9 4.0 %collective-permute-start.4 = (f32[2,4,8,64]{3,2,1,0:T(8,128)S(1)}, f32[2,4,8,64]{3,2,1,0:T(8,128)S(1)}, u32[]{:S(2)}, u32[]{:S(2)}) collective-permute-start(f32[2,4,8,64]{3,2,1,0:T(8,128)S(1)} %get-tuple-element.28), channel_id=1, source_target_pairs={{0,8},{8,16},{16,24},{24,32},{32,40},{40,48},{48,56},{56,64},{64,7... | collective-permute-start | bytes 49160 | tf_op jit(solution)/shard_map/ppermute | solution.py:29
  241.1 0.8 collective-permute-done.4
  242.0 1.9 collective-permute-start.7
  243.9 5.5 %collective-permute-start.6 = (f32[2,16,4,64]{3,2,1,0:T(4,128)S(1)}, f32[2,16,4,64]{3,2,1,0:T(4,128)S(1)}, u32[]{:S(2)}, u32[]{:S(2)}) collective-permute-start(f32[2,16,4,64]{3,2,1,0:T(4,128)S(1)} %get-tuple-element.26), channel_id=1, source_target_pairs={{0,1},{1,2},{2,3},{3,4},{4,5},{5,6},{6,7},{8,9},{9,10},{10,11},{11... | collective-permute-start | bytes 98312 | tf_op jit(solution)/shard_map/ppermute | solution.py:29
  249.5 1.3 collective-permute-done.6
  251.0 1.1 slice_multiply_fusion.4
  252.6 1.1 broadcast_in_dim.64
  253.7 14.4 %all-to-all-start.1 = ((f32[256,8,128]{2,1,0:T(8,128)}), f32[256,8,128]{2,1,0:T(8,128)S(1)}, u32[]{:S(2)}, u32[]{:S(2)}) async-start(f32[256,8,128]{2,1,0:T(8,128)} %broadcast_in_dim.64), calls=%async_computation.1 | async-start | bytes 2097152 | tf_op jit(solution)/shard_map/all_to_all | solution.py:215
  268.7 1.6 squeeze.28
  270.3 28.6 %all-to-all-done.1 = f32[256,8,128]{2,1,0:T(8,128)S(1)} async-done(((f32[256,8,128]{2,1,0:T(8,128)}), f32[256,8,128]{2,1,0:T(8,128)S(1)}, u32[]{:S(2)}, u32[]{:S(2)}) %all-to-all-start.1) | async-done | bytes 1048608 | tf_op jit(solution)/shard_map/all_to_all | solution.py:215
  298.9 3.1 reshape.187
  302.0 4.6 %copy.140 = f32[32,8,2,4,4,32]{5,1,4,3,0,2:T(8,128)S(1)} copy(f32[32,8,2,4,4,32]{5,4,3,2,1,0:T(4,128)} %reshape.187) | data formatting | bytes 2097152 | tf_op jit(solution)/shard_map/reshape | solution.py:216
  306.7 2.0 fusion.342
  308.7 2.0 copy.117
  310.6 3.4 reshape_squeeze.2
  314.0 3.6 %copy.118 = f32[1,32,4,8,4,32]{5,4,3,2,1,0:T(4,128)} copy(f32[1,32,4,8,4,32]{5,3,4,2,1,0:T(8,128)} %get-tuple-element.5) | data formatting | bytes 1048576 | tf_op jit(solution)/shard_map/mul | solution.py:187
  317.6 3.4 mul.529
  321.0 1.9 copy.119
  322.9 3.3 reshape_reshape_squeeze.3
  326.9 0.6 fusion.46
  329.1 2.0 convolution_multiply_fusion
  331.1 1.2 multiply_divide_fusion.1
  333.3 1.5 fusion.253
  335.4 0.6 fusion.67
  336.8 1.8 copy.121
  339.0 1.2 slice_multiply_fusion.6
  340.3 1.3 fusion.137
  342.2 0.8 fusion.118
  (118 shorter events, 9.0 us)
Async XLA Ops:
  0.6 6.1 %copy-start.12 = (f32[1,1,32,8,4,128]{5,4,3,2,1,0:T(4,128)S(1)}, f32[1,1,32,8,4,128]{5,4,3,2,1,0:T(4,128)}, u32[]{:S(2)}) copy-start(f32[1,1,32,8,4,128]{5,4,3,2,1,0:T(4,128)} %param.7) | copy-start | bytes 1572868
  12.5 114.4 %all-to-all-start = ((f32[256,4,8,128]{3,2,1,0:T(8,128)}), f32[256,4,8,128]{3,2,1,0:T(8,128)}, u32[]{:S(2)}, u32[]{:S(2)}) async-start(f32[256,4,8,128]{3,2,1,0:T(8,128)} %pad_maximum_fusion), calls=%async_computation | async-start | bytes 8388608 | tf_op jit(solution)/shard_map/all_to_all | solution.py:249
  29.9 205.3 %copy-start.13 = (s32[128]{0:T(128)}, s32[128]{0:T(128)S(1)}, u32[]{:S(2)}) copy-start(s32[128]{0:T(128)S(1)} %get-tuple-element.41) | copy-start | bytes 1540
  29.9 205.3 %copy-start.15 = (s32[128]{0:T(128)}, s32[128]{0:T(128)S(1)}, u32[]{:S(2)}) copy-start(s32[128]{0:T(128)S(1)} %get-tuple-element.42) | copy-start | bytes 1540
  30.9 202.4 %copy-start = (f32[24,24,128]{2,1,0:T(8,128)}, f32[24,24,128]{2,1,0:T(8,128)S(1)}, u32[]{:S(2)}) copy-start(f32[24,24,128]{2,1,0:T(8,128)S(1)} %and_convert_fusion) | copy-start | bytes 884740
  206.1 10.5 %slice-start = ((f32[4,2,8,2,8,16,8]{5,4,2,6,0,3,1:T(8,128)}), f32[1,2,8,2,8,16,8]{5,4,2,6,0,3,1:T(8,128)S(1)}, s32[]{:S(2)}) async-start(f32[4,2,8,2,8,16,8]{5,4,2,6,0,3,1:T(8,128)} %convolution_bitcast_fusion), calls=%async_computation.2 | async-start | bytes 2097152 | tf_op jit(solution)/shard_map/slice | solution.py:252
  212.5 2.7 copy-start.6
  213.3 5.2 %collective-permute-start = (f32[4,4,16,128]{3,2,1,0:T(8,128)}, f32[4,4,16,128]{3,2,1,0:T(8,128)}, u32[]{:S(2)}, u32[]{:S(2)}) collective-permute-start(f32[4,4,16,128]{3,2,1,0:T(8,128)} %get-tuple-element.17), channel_id=1, source_target_pairs={{0,8},{8,16},{16,24},{24,32},{32,40},{40,48},{48,56},{56,64},{64,7... | collective-permute-start | bytes 393224 | tf_op jit(solution)/shard_map/ppermute | solution.py:29
  215.3 6.0 %collective-permute-start.1 = (f32[4,4,16,128]{3,2,1,0:T(8,128)}, f32[4,4,16,128]{3,2,1,0:T(8,128)}, u32[]{:S(2)}, u32[]{:S(2)}) collective-permute-start(f32[4,4,16,128]{3,2,1,0:T(8,128)} %get-tuple-element.16), channel_id=1, source_target_pairs={{8,0},{16,8},{24,16},{32,24},{40,32},{48,40},{56,48},{64,56},{72,6... | collective-permute-start | bytes 393224 | tf_op jit(solution)/shard_map/ppermute | solution.py:30
  222.3 9.4 %collective-permute-start.3 = (f32[4,24,4,128]{3,2,1,0:T(4,128)S(1)}, f32[4,24,4,128]{3,2,1,0:T(4,128)S(1)}, u32[]{:S(2)}, u32[]{:S(2)}) collective-permute-start(f32[4,24,4,128]{3,2,1,0:T(4,128)S(1)} %get-tuple-element.15), channel_id=1, source_target_pairs={{1,0},{2,1},{3,2},{4,3},{5,4},{6,5},{7,6},{9,8},{10,9},{11,10},{12... | collective-permute-start | bytes 589832 | tf_op jit(solution)/shard_map/ppermute | solution.py:30
  227.3 5.7 %collective-permute-start.2 = (f32[4,24,4,128]{3,2,1,0:T(4,128)S(1)}, f32[4,24,4,128]{3,2,1,0:T(4,128)S(1)}, u32[]{:S(2)}, u32[]{:S(2)}) collective-permute-start(f32[4,24,4,128]{3,2,1,0:T(4,128)S(1)} %get-tuple-element.14), channel_id=1, source_target_pairs={{0,1},{1,2},{2,3},{3,4},{4,5},{5,6},{6,7},{8,9},{9,10},{10,11},{11... | collective-permute-start | bytes 589832 | tf_op jit(solution)/shard_map/ppermute | solution.py:29
  233.5 17.2 %copy-start.2 = (f32[22,22,128]{2,1,0:T(8,128)}, f32[22,22,128]{2,1,0:T(8,128)S(1)}, u32[]{:S(2)}) copy-start(f32[22,22,128]{2,1,0:T(8,128)S(1)} %get-tuple-element.18) | copy-start | bytes 743428
  233.5 18.6 %copy-start.4 = (f32[22,22,128]{2,1,0:T(8,128)}, f32[22,22,128]{2,1,0:T(8,128)S(1)}, u32[]{:S(2)}) copy-start(f32[22,22,128]{2,1,0:T(8,128)S(1)} %get-tuple-element.21) | copy-start | bytes 743428
  233.5 18.6 %copy-start.7 = (f32[22,22,128]{2,1,0:T(8,128)}, f32[22,22,128]{2,1,0:T(8,128)S(1)}, u32[]{:S(2)}) copy-start(f32[22,22,128]{2,1,0:T(8,128)S(1)} %get-tuple-element.19) | copy-start | bytes 743428
  235.6 5.5 %collective-permute-start.5 = (f32[2,4,8,64]{3,2,1,0:T(8,128)S(1)}, f32[2,4,8,64]{3,2,1,0:T(8,128)S(1)}, u32[]{:S(2)}, u32[]{:S(2)}) collective-permute-start(f32[2,4,8,64]{3,2,1,0:T(8,128)S(1)} %get-tuple-element.29), channel_id=1, source_target_pairs={{8,0},{16,8},{24,16},{32,24},{40,32},{48,40},{56,48},{64,56},{72,6... | collective-permute-start | bytes 49160 | tf_op jit(solution)/shard_map/ppermute | solution.py:30
  236.9 5.0 %collective-permute-start.4 = (f32[2,4,8,64]{3,2,1,0:T(8,128)S(1)}, f32[2,4,8,64]{3,2,1,0:T(8,128)S(1)}, u32[]{:S(2)}, u32[]{:S(2)}) collective-permute-start(f32[2,4,8,64]{3,2,1,0:T(8,128)S(1)} %get-tuple-element.28), channel_id=1, source_target_pairs={{0,8},{8,16},{16,24},{24,32},{32,40},{40,48},{48,56},{56,64},{64,7... | collective-permute-start | bytes 49160 | tf_op jit(solution)/shard_map/ppermute | solution.py:29
  242.0 7.5 %collective-permute-start.7 = (f32[2,16,4,64]{3,2,1,0:T(4,128)S(1)}, f32[2,16,4,64]{3,2,1,0:T(4,128)S(1)}, u32[]{:S(2)}, u32[]{:S(2)}) collective-permute-start(f32[2,16,4,64]{3,2,1,0:T(4,128)S(1)} %get-tuple-element.27), channel_id=1, source_target_pairs={{1,0},{2,1},{3,2},{4,3},{5,4},{6,5},{7,6},{9,8},{10,9},{11,10},{12... | collective-permute-start | bytes 98312 | tf_op jit(solution)/shard_map/ppermute | solution.py:30
  243.9 6.8 %collective-permute-start.6 = (f32[2,16,4,64]{3,2,1,0:T(4,128)S(1)}, f32[2,16,4,64]{3,2,1,0:T(4,128)S(1)}, u32[]{:S(2)}, u32[]{:S(2)}) collective-permute-start(f32[2,16,4,64]{3,2,1,0:T(4,128)S(1)} %get-tuple-element.26), channel_id=1, source_target_pairs={{0,1},{1,2},{2,3},{3,4},{4,5},{5,6},{6,7},{8,9},{9,10},{10,11},{11... | collective-permute-start | bytes 98312 | tf_op jit(solution)/shard_map/ppermute | solution.py:29
  250.9 1.4 copy-start.11
  251.0 2.7 copy-start.9
  251.0 2.7 copy-start.10
  253.7 45.2 %all-to-all-start.1 = ((f32[256,8,128]{2,1,0:T(8,128)}), f32[256,8,128]{2,1,0:T(8,128)S(1)}, u32[]{:S(2)}, u32[]{:S(2)}) async-start(f32[256,8,128]{2,1,0:T(8,128)} %broadcast_in_dim.64), calls=%async_computation.1 | async-start | bytes 2097152 | tf_op jit(solution)/shard_map/all_to_all | solution.py:215
  329.1 2.0 copy-start.17
  336.6 3.6 %copy-start.14 = (s32[128]{0:T(128)S(1)}, s32[128]{0:T(128)}, u32[]{:S(2)}) copy-start(s32[128]{0:T(128)} %copy-done.13) | copy-start | bytes 1540
  336.6 3.6 %copy-start.16 = (s32[128]{0:T(128)S(1)}, s32[128]{0:T(128)}, u32[]{:S(2)}) copy-start(s32[128]{0:T(128)} %copy-done.15) | copy-start | bytes 1540
  338.7 3.2 copy-start.1
  338.7 3.2 copy-start.3
  338.7 3.2 copy-start.5
  338.9 3.0 copy-start.8

commit v2 on v1

--- a/solution.py
+++ b/solution.py
@@ -179,14 +179,11 @@
     return field
 
 
-def coarse_solve(f2g, rho2g):
-    sx, ny, nz = f2g.shape
-    f = f2g.reshape(sx, ny * nz)
-    rho2 = rho2g.reshape(sx, ny * nz)
+def coarse_solve(f, rho2, ny, nz):
     rho3 = restrict2d(rho2, ny, nz)
     screens = [None, None, screen_weight * rho2, screen_weight * rho3]
     shapes = [None, None, (ny, nz), (ny // 2, nz // 2)]
-    return vcycle2d(f, 2, screens, shapes).reshape(sx, ny, nz)
+    return vcycle2d(f, 2, screens, shapes)
 
 
 def splat(packed):
@@ -210,12 +207,12 @@
 def gather_all(block, space_count, sub_count):
     channels, nx, ny, nz = block.shape
     devices = space_count * sub_count
-    flat = block.reshape(1, -1, 128)
+    flat = block.reshape(1, channels * nx, ny * nz)
     sent = jnp.broadcast_to(flat, (devices,) + flat.shape[1:])
     every = lax.all_to_all(sent, ("space", "sub"), 0, 0, tiled=True)
-    every = every.reshape(space_count, sub_count, channels, nx, ny, nz)
-    every = every.transpose(2, 0, 3, 1, 4, 5)
-    return every.reshape(channels, space_count * nx, sub_count * ny, nz)
+    every = every.reshape(space_count, sub_count, channels, nx, ny * nz)
+    every = every.transpose(2, 0, 3, 1, 4)
+    return every.reshape(channels, space_count * nx, sub_count * ny * nz)
 
 
 def to_grid(sums):
@@ -290,15 +287,14 @@
 
     rho2 = restrict(rho1)
     both2 = gather_all(jnp.stack([f2, rho2]), space_count, sub_count)
-    f2g, rho2g = both2[0], both2[1]
-    c2g = coarse_solve(f2g, rho2g)
+    c2g = coarse_solve(both2[0], both2[1], sub_count * ny2, nz2)
     hc2 = (hu1 + 1) // 2
-    c2p = jnp.pad(c2g, ((hc2, hc2), (hc2, hc2), (0, 0)))
+    c2p = jnp.pad(c2g, ((hc2, hc2), (hc2 * nz2, hc2 * nz2)))
     c2 = lax.dynamic_slice(
         c2p,
-        (lax.axis_index("space") * nx2, lax.axis_index("sub") * ny2, 0),
-        (nx2 + 2 * hc2, ny2 + 2 * hc2, nz2),
-    )
+        (lax.axis_index("space") * nx2, lax.axis_index("sub") * ny2 * nz2),
+        (nx2 + 2 * hc2, (ny2 + 2 * hc2) * nz2),
+    ).reshape(nx2 + 2 * hc2, ny2 + 2 * hc2, nz2)
 
     u1 = u1 + crop(prolong(c2), 2 * hc2, hu1)
     hcur = hu1

time: 349 us -> 326 us (0.934)
  local copies, waits for them, and re-layouts: 82.8 us -> 60.7 us
    reshape x3 -> x0, local copies, waits for them, and re-layouts: 9.59 us -> none  [the longest x2 7.76 us: gather_all(): every = every.reshape(space_count, sub_count, channels, nx, ny, nz)]
    mul x2 -> x1, local copies, waits for them, and re-layouts: 6.96 us -> 0.05 us  [coarse_solve(): screens = [None, None, screen_weight * rho2, screen_weight * rho3]]
    slice x2, local copies, waits for them, and re-layouts: 3.9 us -> 0.12 us  [on_device(): c2g = coarse_solve(both2[0], both2[1], sub_count * ny2, nz2)]
where the time goes in v2:
time: 326 us; the launch traced here: 320 us
  waiting for transfers between devices  130 us (40%)
  local copies, waits for them, and re-layouts  60.7 us (19%)
  starting transfers between devices  56.3 us (17%)
  matrix products  46.3 us (14%)
  other arithmetic  25.6 us (8%)
    all_to_all x1, waiting for transfers between devices, on_device(): received = lax.all_to_all(packed, ('space', 'sub'), 0, 0, tiled=True)  96.1 us
    dot_general x1, matrix products, splat(): jnp.einsum('tbs,tas->tba', loaded, planar, precision=lax.Precision.HIGH)  31 us
    all_to_all x1, waiting for transfers between devices, gather_all(): every = lax.all_to_all(sent, ('space', 'sub'), 0, 0, tiled=True)  28.1 us
    all_to_all x1, starting transfers between devices, on_device(): received = lax.all_to_all(packed, ('space', 'sub'), 0, 0, tiled=True)  17 us
    all_to_all x1, starting transfers between devices, gather_all(): every = lax.all_to_all(sent, ('space', 'sub'), 0, 0, tiled=True)  15.3 us
    ppermute x4, starting transfers between devices, exchange(): before = lax.ppermute(last, axis, up)  14.5 us
    dot_general x2, local copies, waits for them, and re-layouts, splat(): jnp.einsum('tk,tba->kba', onehot, partials, precision=lax.Precision.HIGH)  14.1 us
    ppermute x4, starting transfers between devices, exchange(): after = lax.ppermute(first, axis, down)  9.45 us
  transfers between devices with their start and end apart: 10, of which 7 were waited for; matrix products, arithmetic and copies ran while one was open for 2% of the time, Pallas kernels for 0%

profile of v2, /device:TPU:1, one launch (start us, length us, event | category | flops | bytes accessed | tf_op | source)
XLA Modules:
  0.0 320.4 jit_solution(14101935232855549382)
XLA Ops:
  0.6 0.8 convert_element_type.133
  1.6 2.0 copy.88
  3.6 0.9 copy.112
  4.4 0.3 fusion.81
  4.8 2.0 copy.87
  6.8 1.1 maximum_multiply_fusion
  7.9 1.2 broadcast_in_dim.62
  9.2 3.3 %pad_maximum_fusion = f32[256,4,8,128]{3,2,1,0:T(8,128)} fusion(f32[256,4,1,128]{3,2,1,0:T(1,128)S(1)} %broadcast_in_dim.62, f32[256,4,4,128]{3,2,1,0:T(4,128)S(1)} %maximum_multiply_fusion, f32[256,4,3,128]{3,2,1,0:T(4,128)S(1)} %bitcast.155), kind=kLoop, calls=%fused_computation.10 | loop fusion | flops 2097152 | bytes 8388608 | tf_op jit(solution)/shard_map/concatenate | solution.py:243
  12.5 17.0 %all-to-all-start = ((f32[256,4,8,128]{3,2,1,0:T(8,128)}), f32[256,4,8,128]{3,2,1,0:T(8,128)}, u32[]{:S(2)}, u32[]{:S(2)}) async-start(f32[256,4,8,128]{3,2,1,0:T(8,128)} %pad_maximum_fusion), calls=%async_computation | async-start | bytes 8388608 | tf_op jit(solution)/shard_map/all_to_all | solution.py:246
  29.7 0.8 fusion.121
  30.5 96.1 %all-to-all-done = f32[256,4,8,128]{3,2,1,0:T(8,128)} async-done(((f32[256,4,8,128]{3,2,1,0:T(8,128)}), f32[256,4,8,128]{3,2,1,0:T(8,128)}, u32[]{:S(2)}, u32[]{:S(2)}) %all-to-all-start) | async-done | bytes 4194336 | tf_op jit(solution)/shard_map/all_to_all | solution.py:246
  126.6 2.6 slice.777
  129.3 6.8 %fusion.341 = (f32[1024,1,128]{2,1,0:T(1,128)S(1)}, f32[1024,1,128]{2,1,0:T(1,128)}, f32[1024,1,128]{2,1,0:T(1,128)}) fusion(f32[1024,8,128]{2,1,0:T(8,128)} %bitcast.5), kind=kLoop, calls=%fused_computation.526 | loop fusion | bytes 3145728 | tf_op jit(solution)/shard_map/slice | solution.py:193
  136.1 2.6 slice.778
  138.7 0.7 fusion.82
  139.5 1.1 copy.93
  140.6 6.0 %subtract_maximum_fusion.2 = (f32[1024,8,128]{2,1,0:T(8,128)}, f32[1024,8,128]{2,1,0:T(8,128)}, f32[1024,8,128]{2,1,0:T(8,128)}) fusion(f32[8]{0:T(128)S(1)} %iota_add_fusion, f32[1024,128]{1,0:T(8,128)S(1)} %bitcast.159, f32[1024,128]{1,0:T(8,128)} %bitcast.161, f32[1024,128]{1,0:T(8,128)} %bitcast.160), kind=kLoop, calls=%fused_computation.13 | loop fusion | flops 12582912 | bytes 14155808 | tf_op jit(solution)/shard_map/max | solution.py:193
  146.5 31.0 %fusion.7 = f32[32,64,1024]{1,0,2:T(8,128)} fusion(f32[1024,8,128]{2,1,0:T(8,128)} %get-tuple-element.34, f32[1024,8,128]{2,1,0:T(8,128)} %get-tuple-element.33, f32[1024,8,128]{2,1,0:T(8,128)} %get-tuple-element.32, f32[1024,4,128]{2,1,0:T(4,128)S(1)} %slice.778), kind=kOutput, calls=%fused_computation.7 | convolution fusion | flops 1623195648 | bytes 23068672 | tf_op jit(solution)/shard_map/tbs,tas->tba/dot_general | solution.py:198
  177.6 13.0 %copy.94 = f32[32,64,1024]{2,1,0:T(8,128)} copy(f32[32,64,1024]{1,0,2:T(8,128)} %fusion.7) | data formatting | bytes 16777216 | tf_op jit(solution)/shard_map/tk,tba->kba/dot_general | solution.py:203
  190.5 8.2 %convolution_bitcast_fusion = f32[4,2,8,2,8,16,8]{5,4,2,6,0,3,1:T(8,128)} fusion(pred[2,2,16,1024,1,1,1]{3,2,6,5,4,1,0:T(8,128)(4,1)S(1)} %bitcast.173, f32[4,8,8,8,1024,1,1]{4,3,2,1,0,6,5:T(8,128)} %bitcast.154), kind=kOutput, calls=%fused_computation.22 | convolution fusion | flops 805306368 | bytes 8978432 | tf_op jit(solution)/shard_map/tk,tba->kba/dot_general | solution.py:203
  198.8 7.0 %copy.95 = f32[4,2,8,2,8,16,8]{6,5,4,3,2,1,0:T(8,128)} copy(f32[4,2,8,2,8,16,8]{5,4,2,6,0,3,1:T(8,128)} %convolution_bitcast_fusion) | data formatting | bytes 1048576 | tf_op jit(solution)/shard_map/transpose | solution.py:220
  205.7 6.5 %reshape.178 = f32[4,16,16,128]{3,2,1,0:T(8,128)S(1)} reshape(f32[4,2,8,2,8,16,8]{6,5,4,3,2,1,0:T(8,128)} %copy.95) | data formatting | bytes 1048576 | tf_op jit(solution)/shard_map/reshape | solution.py:220
  212.2 0.8 fusion.344
  213.0 1.9 collective-permute-start
  215.0 1.3 collective-permute-start.1
  216.3 0.7 copy.98
  216.9 1.0 dot_general.57
  218.3 0.9 constant_dynamic-update-slice_fusion.2
  219.2 1.1 constant_dynamic-update-slice_fusion.1
  220.3 0.7 collective-permute-done.1
  221.0 0.9 constant_dynamic-update-slice_fusion
  222.0 5.0 %collective-permute-start.3 = (f32[4,24,4,128]{3,2,1,0:T(4,128)S(1)}, f32[4,24,4,128]{3,2,1,0:T(4,128)S(1)}, u32[]{:S(2)}, u32[]{:S(2)}) collective-permute-start(f32[4,24,4,128]{3,2,1,0:T(4,128)S(1)} %get-tuple-element.15), channel_id=1, source_target_pairs={{1,0},{2,1},{3,2},{4,3},{5,4},{6,5},{7,6},{9,8},{10,9},{11,10},{12... | collective-permute-start | bytes 589832 | tf_op jit(solution)/shard_map/ppermute | solution.py:30
  226.9 3.1 collective-permute-start.2
  230.0 1.4 collective-permute-done.3
  231.4 1.2 collective-permute-done.2
  233.2 0.3 fusion.96
  233.6 0.3 copy-done.1
  234.4 1.3 collective-permute-start.5
  235.7 4.0 %collective-permute-start.4 = (f32[2,4,8,64]{3,2,1,0:T(8,128)S(1)}, f32[2,4,8,64]{3,2,1,0:T(8,128)S(1)}, u32[]{:S(2)}, u32[]{:S(2)}) collective-permute-start(f32[2,4,8,64]{3,2,1,0:T(8,128)S(1)} %get-tuple-element.28), channel_id=1, source_target_pairs={{0,8},{8,16},{16,24},{24,32},{32,40},{40,48},{48,56},{56,64},{64,7... | collective-permute-start | bytes 49160 | tf_op jit(solution)/shard_map/ppermute | solution.py:29
  239.9 0.8 collective-permute-done.4
  240.8 1.9 collective-permute-start.7
  242.7 5.5 %collective-permute-start.6 = (f32[2,16,4,64]{3,2,1,0:T(4,128)S(1)}, f32[2,16,4,64]{3,2,1,0:T(4,128)S(1)}, u32[]{:S(2)}, u32[]{:S(2)}) collective-permute-start(f32[2,16,4,64]{3,2,1,0:T(4,128)S(1)} %get-tuple-element.26), channel_id=1, source_target_pairs={{0,1},{1,2},{2,3},{3,4},{4,5},{5,6},{6,7},{8,9},{9,10},{10,11},{11... | collective-permute-start | bytes 98312 | tf_op jit(solution)/shard_map/ppermute | solution.py:29
  248.3 1.3 collective-permute-done.6
  249.8 1.1 slice_multiply_fusion.4
  251.4 1.1 broadcast_in_dim.64
  252.5 15.3 %all-to-all-start.1 = ((f32[256,8,128]{2,1,0:T(8,128)}), f32[256,8,128]{2,1,0:T(8,128)}, u32[]{:S(2)}, u32[]{:S(2)}) async-start(f32[256,8,128]{2,1,0:T(8,128)} %broadcast_in_dim.64), calls=%async_computation.1 | async-start | bytes 2097152 | tf_op jit(solution)/shard_map/all_to_all | solution.py:212
  267.8 1.6 squeeze.33
  269.5 28.1 %all-to-all-done.1 = f32[256,8,128]{2,1,0:T(8,128)} async-done(((f32[256,8,128]{2,1,0:T(8,128)}), f32[256,8,128]{2,1,0:T(8,128)}, u32[]{:S(2)}, u32[]{:S(2)}) %all-to-all-start.1) | async-done | bytes 1048608 | tf_op jit(solution)/shard_map/all_to_all | solution.py:212
  297.6 1.4 copy.103
  299.6 1.4 reduce_sum.99
  301.2 0.6 fusion.46
  301.9 1.4 fusion.55
  303.3 1.3 reshape.184
  304.6 1.3 reduce_sum.98
  306.0 2.2 convolution_multiply_fusion
  308.2 1.2 multiply_divide_fusion
  310.4 1.5 fusion.254
  311.9 1.0 broadcast_in_dim.67
  312.8 1.4 reshape.185
  314.3 0.6 fusion.67
  315.0 0.6 fusion.79
  316.0 1.2 slice_multiply_fusion.6
  317.2 1.2 fusion.138
  319.1 0.8 fusion.119
  (97 shorter events, 5.4 us)
Async XLA Ops:
  0.6 6.1 %copy-start.7 = (f32[1,1,32,8,4,128]{5,4,3,2,1,0:T(4,128)S(1)}, f32[1,1,32,8,4,128]{5,4,3,2,1,0:T(4,128)}, u32[]{:S(2)}) copy-start(f32[1,1,32,8,4,128]{5,4,3,2,1,0:T(4,128)} %param.7) | copy-start | bytes 1572868
  12.5 114.1 %all-to-all-start = ((f32[256,4,8,128]{3,2,1,0:T(8,128)}), f32[256,4,8,128]{3,2,1,0:T(8,128)}, u32[]{:S(2)}, u32[]{:S(2)}) async-start(f32[256,4,8,128]{3,2,1,0:T(8,128)} %pad_maximum_fusion), calls=%async_computation | async-start | bytes 8388608 | tf_op jit(solution)/shard_map/all_to_all | solution.py:246
  205.7 10.5 %slice-start = ((f32[4,2,8,2,8,16,8]{5,4,2,6,0,3,1:T(8,128)}), f32[1,2,8,2,8,16,8]{5,4,2,6,0,3,1:T(8,128)S(1)}, s32[]{:S(2)}) async-start(f32[4,2,8,2,8,16,8]{5,4,2,6,0,3,1:T(8,128)} %convolution_bitcast_fusion), calls=%async_computation.2 | async-start | bytes 2097152 | tf_op jit(solution)/shard_map/slice | solution.py:249
  212.2 2.8 copy-start
  213.0 5.3 %collective-permute-start = (f32[4,4,16,128]{3,2,1,0:T(8,128)}, f32[4,4,16,128]{3,2,1,0:T(8,128)}, u32[]{:S(2)}, u32[]{:S(2)}) collective-permute-start(f32[4,4,16,128]{3,2,1,0:T(8,128)} %get-tuple-element.17), channel_id=1, source_target_pairs={{0,8},{8,16},{16,24},{24,32},{32,40},{40,48},{48,56},{56,64},{64,7... | collective-permute-start | bytes 393224 | tf_op jit(solution)/shard_map/ppermute | solution.py:29
  215.0 6.0 %collective-permute-start.1 = (f32[4,4,16,128]{3,2,1,0:T(8,128)}, f32[4,4,16,128]{3,2,1,0:T(8,128)}, u32[]{:S(2)}, u32[]{:S(2)}) collective-permute-start(f32[4,4,16,128]{3,2,1,0:T(8,128)} %get-tuple-element.16), channel_id=1, source_target_pairs={{8,0},{16,8},{24,16},{32,24},{40,32},{48,40},{56,48},{64,56},{72,6... | collective-permute-start | bytes 393224 | tf_op jit(solution)/shard_map/ppermute | solution.py:30
  222.0 9.4 %collective-permute-start.3 = (f32[4,24,4,128]{3,2,1,0:T(4,128)S(1)}, f32[4,24,4,128]{3,2,1,0:T(4,128)S(1)}, u32[]{:S(2)}, u32[]{:S(2)}) collective-permute-start(f32[4,24,4,128]{3,2,1,0:T(4,128)S(1)} %get-tuple-element.15), channel_id=1, source_target_pairs={{1,0},{2,1},{3,2},{4,3},{5,4},{6,5},{7,6},{9,8},{10,9},{11,10},{12... | collective-permute-start | bytes 589832 | tf_op jit(solution)/shard_map/ppermute | solution.py:30
  226.9 5.7 %collective-permute-start.2 = (f32[4,24,4,128]{3,2,1,0:T(4,128)S(1)}, f32[4,24,4,128]{3,2,1,0:T(4,128)S(1)}, u32[]{:S(2)}, u32[]{:S(2)}) collective-permute-start(f32[4,24,4,128]{3,2,1,0:T(4,128)S(1)} %get-tuple-element.14), channel_id=1, source_target_pairs={{0,1},{1,2},{2,3},{3,4},{4,5},{5,6},{6,7},{8,9},{9,10},{10,11},{11... | collective-permute-start | bytes 589832 | tf_op jit(solution)/shard_map/ppermute | solution.py:29
  233.2 0.7 copy-start.1
  234.4 5.5 %collective-permute-start.5 = (f32[2,4,8,64]{3,2,1,0:T(8,128)S(1)}, f32[2,4,8,64]{3,2,1,0:T(8,128)S(1)}, u32[]{:S(2)}, u32[]{:S(2)}) collective-permute-start(f32[2,4,8,64]{3,2,1,0:T(8,128)S(1)} %get-tuple-element.29), channel_id=1, source_target_pairs={{8,0},{16,8},{24,16},{32,24},{40,32},{48,40},{56,48},{64,56},{72,6... | collective-permute-start | bytes 49160 | tf_op jit(solution)/shard_map/ppermute | solution.py:30
  235.7 5.0 %collective-permute-start.4 = (f32[2,4,8,64]{3,2,1,0:T(8,128)S(1)}, f32[2,4,8,64]{3,2,1,0:T(8,128)S(1)}, u32[]{:S(2)}, u32[]{:S(2)}) collective-permute-start(f32[2,4,8,64]{3,2,1,0:T(8,128)S(1)} %get-tuple-element.28), channel_id=1, source_target_pairs={{0,8},{8,16},{16,24},{24,32},{32,40},{40,48},{48,56},{56,64},{64,7... | collective-permute-start | bytes 49160 | tf_op jit(solution)/shard_map/ppermute | solution.py:29
  240.8 7.5 %collective-permute-start.7 = (f32[2,16,4,64]{3,2,1,0:T(4,128)S(1)}, f32[2,16,4,64]{3,2,1,0:T(4,128)S(1)}, u32[]{:S(2)}, u32[]{:S(2)}) collective-permute-start(f32[2,16,4,64]{3,2,1,0:T(4,128)S(1)} %get-tuple-element.27), channel_id=1, source_target_pairs={{1,0},{2,1},{3,2},{4,3},{5,4},{6,5},{7,6},{9,8},{10,9},{11,10},{12... | collective-permute-start | bytes 98312 | tf_op jit(solution)/shard_map/ppermute | solution.py:30
  242.7 6.8 %collective-permute-start.6 = (f32[2,16,4,64]{3,2,1,0:T(4,128)S(1)}, f32[2,16,4,64]{3,2,1,0:T(4,128)S(1)}, u32[]{:S(2)}, u32[]{:S(2)}) collective-permute-start(f32[2,16,4,64]{3,2,1,0:T(4,128)S(1)} %get-tuple-element.26), channel_id=1, source_target_pairs={{0,1},{1,2},{2,3},{3,4},{4,5},{5,6},{6,7},{8,9},{9,10},{10,11},{11... | collective-permute-start | bytes 98312 | tf_op jit(solution)/shard_map/ppermute | solution.py:29
  249.7 1.4 copy-start.6
  249.8 1.2 copy-start.3
  249.8 1.3 copy-start.5
  252.5 45.1 %all-to-all-start.1 = ((f32[256,8,128]{2,1,0:T(8,128)}), f32[256,8,128]{2,1,0:T(8,128)}, u32[]{:S(2)}, u32[]{:S(2)}) async-start(f32[256,8,128]{2,1,0:T(8,128)} %broadcast_in_dim.64), calls=%async_computation.1 | async-start | bytes 2097152 | tf_op jit(solution)/shard_map/all_to_all | solution.py:212
  306.0 2.3 copy-start.8
  314.3 2.9 copy-start.4
  314.9 3.9 %copy-start.2 = (f32[22,22,128]{2,1,0:T(8,128)S(1)}, f32[22,22,128]{2,1,0:T(8,128)}, u32[]{:S(2)}) copy-start(f32[22,22,128]{2,1,0:T(8,128)} %copy-done.1) | copy-start | bytes 743428

commit v3 on v2

--- a/solution.py
+++ b/solution.py
@@ -19,17 +19,33 @@
 
 
 def exchange(x, width, dim_x, dim_y):
-    for axis, dim in (("space", dim_x), ("sub", dim_y)):
-        devices = lax.axis_size(axis)
-        length = x.shape[dim]
-        up = [(i, i + 1) for i in range(devices - 1)]
-        down = [(j, i) for i, j in up]
-        last = lax.slice_in_dim(x, length - width, length, axis=dim)
-        first = lax.slice_in_dim(x, 0, width, axis=dim)
-        before = lax.ppermute(last, axis, up)
-        after = lax.ppermute(first, axis, down)
-        x = jnp.concatenate([before, x, after], axis=dim)
-    return x
+    spaces = lax.axis_size("space")
+    subs = lax.axis_size("sub")
+
+    def part(piece, side, dim):
+        length = piece.shape[dim]
+        if side < 0:
+            return lax.slice_in_dim(piece, length - width, length, axis=dim)
+        if side > 0:
+            return lax.slice_in_dim(piece, 0, width, axis=dim)
+        return piece
+
+    rows = []
+    for rx in (-1, 0, 1):
+        columns = []
+        for ry in (-1, 0, 1):
+            piece = part(part(x, rx, dim_x), ry, dim_y)
+            if rx or ry:
+                perm = [
+                    (s * subs + b, (s - rx) * subs + (b - ry))
+                    for s in range(spaces)
+                    for b in range(subs)
+                    if 0 <= s - rx < spaces and 0 <= b - ry < subs
+                ]
+                piece = lax.ppermute(piece, ("space", "sub"), perm)
+            columns.append(piece)
+        rows.append(jnp.concatenate(columns, axis=dim_y))
+    return jnp.concatenate(rows, axis=dim_x)
 
 
 def crop(x, h_from, h_to):

time: 326 us -> 347 us (1.064)
  starting transfers between devices: 56.3 us -> 79.5 us
  waiting for transfers between devices: 130 us -> 125 us
    ppermute x8 -> x16, starting transfers between devices: 24 us -> 48 us  [exchange(): piece = lax.ppermute(piece, ('space', 'sub'), perm)]
    ppermute x8 -> x16, waiting for transfers between devices: 5.38 us -> 1.69 us  [exchange(): piece = lax.ppermute(piece, ('space', 'sub'), perm)]
  transfers between devices with their start and end apart: 10 -> 18, of which waited for: 7 -> 4; matrix products, arithmetic and copies ran while one was open for 2% -> 2% of each run, Pallas kernels for 0% -> 0%
where the time goes in v3:
time: 347 us; the launch traced here: 341 us
  waiting for transfers between devices  125 us (36%)
  starting transfers between devices  79.5 us (23%)
  local copies, waits for them, and re-layouts  59.4 us (17%)
  matrix products  47 us (14%)
  other arithmetic  27.4 us (8%)
    all_to_all x1, waiting for transfers between devices, on_device(): received = lax.all_to_all(packed, ('space', 'sub'), 0, 0, tiled=True)  95.6 us
    ppermute x16, starting transfers between devices, exchange(): piece = lax.ppermute(piece, ('space', 'sub'), perm)  48 us
    dot_general x1, matrix products, splat(): jnp.einsum('tbs,tas->tba', loaded, planar, precision=lax.Precision.HIGH)  31 us
    all_to_all x1, waiting for transfers between devices, gather_all(): every = lax.all_to_all(sent, ('space', 'sub'), 0, 0, tiled=True)  28.1 us
    all_to_all x1, starting transfers between devices, on_device(): received = lax.all_to_all(packed, ('space', 'sub'), 0, 0, tiled=True)  17 us
    all_to_all x1, starting transfers between devices, gather_all(): every = lax.all_to_all(sent, ('space', 'sub'), 0, 0, tiled=True)  14.6 us
    dot_general x2, local copies, waits for them, and re-layouts, splat(): jnp.einsum('tk,tba->kba', onehot, partials, precision=lax.Precision.HIGH)  14.1 us
    dot_general x1, matrix products, splat(): jnp.einsum('tk,tba->kba', onehot, partials, precision=lax.Precision.HIGH)  8.26 us
  transfers between devices with their start and end apart: 18, of which 4 were waited for; matrix products, arithmetic and copies ran while one was open for 2% of the time, Pallas kernels for 0%

profile of v3, /device:TPU:1, one launch (start us, length us, event | category | flops | bytes accessed | tf_op | source)
XLA Modules:
  0.0 340.8 jit_solution(13423866431930734297)
XLA Ops:
  0.6 0.8 convert_element_type.133
  1.6 2.0 copy.88
  3.6 0.9 copy.112
  4.8 2.0 copy.87
  6.8 1.1 maximum_multiply_fusion
  7.9 1.2 broadcast_in_dim.62
  9.2 3.4 pad_maximum_fusion
  12.6 17.0 %all-to-all-start = ((f32[256,4,8,128]{3,2,1,0:T(8,128)}), f32[256,4,8,128]{3,2,1,0:T(8,128)}, u32[]{:S(2)}, u32[]{:S(2)}) async-start(f32[256,4,8,128]{3,2,1,0:T(8,128)} %pad_maximum_fusion), calls=%async_computation | async-start | bytes 8388608 | tf_op jit(solution)/shard_map/all_to_all | solution.py:262
  30.2 0.8 fusion.121
  31.1 95.6 %all-to-all-done = f32[256,4,8,128]{3,2,1,0:T(8,128)} async-done(((f32[256,4,8,128]{3,2,1,0:T(8,128)}), f32[256,4,8,128]{3,2,1,0:T(8,128)}, u32[]{:S(2)}, u32[]{:S(2)}) %all-to-all-start) | async-done | bytes 4194336 | tf_op jit(solution)/shard_map/all_to_all | solution.py:262
  126.7 2.6 slice.825
  129.3 6.9 %fusion.347 = (f32[1024,1,128]{2,1,0:T(1,128)S(1)}, f32[1024,1,128]{2,1,0:T(1,128)}, f32[1024,1,128]{2,1,0:T(1,128)}) fusion(f32[1024,8,128]{2,1,0:T(8,128)} %bitcast.5), kind=kLoop, calls=%fused_computation.540 | loop fusion | bytes 3145728 | tf_op jit(solution)/shard_map/slice | solution.py:209
  136.2 2.6 slice.826
  138.9 0.7 fusion.82
  139.6 1.1 copy.93
  140.7 6.0 %subtract_maximum_fusion.2 = (f32[1024,8,128]{2,1,0:T(8,128)}, f32[1024,8,128]{2,1,0:T(8,128)}, f32[1024,8,128]{2,1,0:T(8,128)}) fusion(f32[8]{0:T(128)S(1)} %iota_add_fusion, f32[1024,128]{1,0:T(8,128)S(1)} %bitcast.159, f32[1024,128]{1,0:T(8,128)} %bitcast.161, f32[1024,128]{1,0:T(8,128)} %bitcast.160), kind=kLoop, calls=%fused_computation.13 | loop fusion | flops 12582912 | bytes 14155808 | tf_op jit(solution)/shard_map/max | solution.py:209
  146.7 31.0 %fusion.7 = f32[32,64,1024]{1,0,2:T(8,128)} fusion(f32[1024,8,128]{2,1,0:T(8,128)} %get-tuple-element.42, f32[1024,8,128]{2,1,0:T(8,128)} %get-tuple-element.41, f32[1024,8,128]{2,1,0:T(8,128)} %get-tuple-element.40, f32[1024,4,128]{2,1,0:T(4,128)S(1)} %slice.826), kind=kOutput, calls=%fused_computation.7 | convolution fusion | flops 1623195648 | bytes 23068672 | tf_op jit(solution)/shard_map/tbs,tas->tba/dot_general | solution.py:214
  177.8 13.0 %copy.94 = f32[32,64,1024]{2,1,0:T(8,128)} copy(f32[32,64,1024]{1,0,2:T(8,128)} %fusion.7) | data formatting | bytes 16777216 | tf_op jit(solution)/shard_map/tk,tba->kba/dot_general | solution.py:219
  190.8 8.3 %convolution_bitcast_fusion = f32[4,2,8,2,8,16,8]{5,4,2,6,0,3,1:T(8,128)} fusion(pred[2,2,16,1024,1,1,1]{3,2,6,5,4,1,0:T(8,128)(4,1)S(1)} %bitcast.173, f32[4,8,8,8,1024,1,1]{4,3,2,1,0,6,5:T(8,128)} %bitcast.154), kind=kOutput, calls=%fused_computation.22 | convolution fusion | flops 805306368 | bytes 8978432 | tf_op jit(solution)/shard_map/tk,tba->kba/dot_general | solution.py:219
  199.0 7.0 %copy.95 = f32[4,2,8,2,8,16,8]{6,5,4,3,2,1,0:T(8,128)} copy(f32[4,2,8,2,8,16,8]{5,4,2,6,0,3,1:T(8,128)} %convolution_bitcast_fusion) | data formatting | bytes 1048576 | tf_op jit(solution)/shard_map/transpose | solution.py:236
  206.1 6.5 %reshape.178 = f32[4,16,16,128]{3,2,1,0:T(8,128)S(1)} reshape(f32[4,2,8,2,8,16,8]{6,5,4,3,2,1,0:T(8,128)} %copy.95) | data formatting | bytes 1048576 | tf_op jit(solution)/shard_map/reshape | solution.py:236
  212.6 0.7 fusion.349
  213.3 0.7 fusion.350
  214.0 0.8 fusion.351
  214.8 1.3 collective-permute-start.7
  216.1 1.3 collective-permute-start.6
  217.4 1.3 collective-permute-start.5
  218.7 2.3 collective-permute-start.4
  221.0 3.6 %collective-permute-start.3 = (f32[4,16,4,128]{3,2,1,0:T(4,128)}, f32[4,16,4,128]{3,2,1,0:T(4,128)}, u32[]{:S(2)}, u32[]{:S(2)}) collective-permute-start(f32[4,16,4,128]{3,2,1,0:T(4,128)} %get-tuple-element.20), channel_id=1, source_target_pairs={{0,1},{1,2},{2,3},{3,4},{4,5},{5,6},{6,7},{8,9},{9,10},{10,11},{11... | collective-permute-start | bytes 393224 | tf_op jit(solution)/shard_map/ppermute | solution.py:45
  224.6 0.7 copy.98
  225.2 1.0 dot_general.57
  226.2 0.8 convolution_reduce_fusion
  227.2 5.1 %collective-permute-start.2 = (f32[4,4,4,128]{3,2,1,0:T(4,128)}, f32[4,4,4,128]{3,2,1,0:T(4,128)S(1)}, u32[]{:S(2)}, u32[]{:S(2)}) collective-permute-start(f32[4,4,4,128]{3,2,1,0:T(4,128)} %get-tuple-element.17), channel_id=1, source_target_pairs={{1,8},{2,9},{3,10},{4,11},{5,12},{6,13},{7,14},{9,16},{10,17},{11,... | collective-permute-start | bytes 98312 | tf_op jit(solution)/shard_map/ppermute | solution.py:45
  232.3 3.9 %collective-permute-start.1 = (f32[4,4,16,128]{3,2,1,0:T(8,128)}, f32[4,4,16,128]{3,2,1,0:T(8,128)S(1)}, u32[]{:S(2)}, u32[]{:S(2)}) collective-permute-start(f32[4,4,16,128]{3,2,1,0:T(8,128)} %get-tuple-element.18), channel_id=1, source_target_pairs={{0,8},{1,9},{2,10},{3,11},{4,12},{5,13},{6,14},{7,15},{8,16},{9,17... | collective-permute-start | bytes 393224 | tf_op jit(solution)/shard_map/ppermute | solution.py:45
  236.2 5.6 %collective-permute-start = (f32[4,4,4,128]{3,2,1,0:T(4,128)S(1)}, f32[4,4,4,128]{3,2,1,0:T(4,128)S(1)}, u32[]{:S(2)}, u32[]{:S(2)}) collective-permute-start(f32[4,4,4,128]{3,2,1,0:T(4,128)S(1)} %get-tuple-element.14), channel_id=1, source_target_pairs={{0,9},{1,10},{2,11},{3,12},{4,13},{5,14},{6,15},{8,17},{9,18},{10,... | collective-permute-start | bytes 98312 | tf_op jit(solution)/shard_map/ppermute | solution.py:45
  242.0 0.8 collective-permute-done
  242.9 1.4 maximum_maximum_fusion
  246.0 1.3 collective-permute-start.15
  247.3 1.3 collective-permute-start.13
  248.6 4.3 %collective-permute-start.10 = (f32[2,4,4,64]{3,2,1,0:T(4,128)S(1)}, f32[2,4,4,64]{3,2,1,0:T(4,128)S(1)}, u32[]{:S(2)}, u32[]{:S(2)}) collective-permute-start(f32[2,4,4,64]{3,2,1,0:T(4,128)S(1)} %get-tuple-element.31), channel_id=1, source_target_pairs={{1,8},{2,9},{3,10},{4,11},{5,12},{6,13},{7,14},{9,16},{10,17},{11,... | collective-permute-start | bytes 24584 | tf_op jit(solution)/shard_map/ppermute | solution.py:45
  252.9 1.3 collective-permute-start.14
  254.2 1.9 collective-permute-start.12
  256.1 3.6 %collective-permute-start.11 = (f32[2,8,4,64]{3,2,1,0:T(4,128)S(1)}, f32[2,8,4,64]{3,2,1,0:T(4,128)S(1)}, u32[]{:S(2)}, u32[]{:S(2)}) collective-permute-start(f32[2,8,4,64]{3,2,1,0:T(4,128)S(1)} %get-tuple-element.36), channel_id=1, source_target_pairs={{0,1},{1,2},{2,3},{3,4},{4,5},{5,6},{6,7},{8,9},{9,10},{10,11},{11... | collective-permute-start | bytes 49160 | tf_op jit(solution)/shard_map/ppermute | solution.py:45
  259.8 5.8 %collective-permute-start.9 = (f32[2,4,8,64]{3,2,1,0:T(8,128)S(1)}, f32[2,4,8,64]{3,2,1,0:T(8,128)S(1)}, u32[]{:S(2)}, u32[]{:S(2)}) collective-permute-start(f32[2,4,8,64]{3,2,1,0:T(8,128)S(1)} %get-tuple-element.34), channel_id=1, source_target_pairs={{0,8},{1,9},{2,10},{3,11},{4,12},{5,13},{6,14},{7,15},{8,16},{9,17... | collective-permute-start | bytes 49160 | tf_op jit(solution)/shard_map/ppermute | solution.py:45
  265.6 4.1 %collective-permute-start.8 = (f32[2,4,4,64]{3,2,1,0:T(4,128)S(1)}, f32[2,4,4,64]{3,2,1,0:T(4,128)S(1)}, u32[]{:S(2)}, u32[]{:S(2)}) collective-permute-start(f32[2,4,4,64]{3,2,1,0:T(4,128)S(1)} %get-tuple-element.30), channel_id=1, source_target_pairs={{0,9},{1,10},{2,11},{3,12},{4,13},{5,14},{6,15},{8,17},{9,18},{10,... | collective-permute-start | bytes 24584 | tf_op jit(solution)/shard_map/ppermute | solution.py:45
  269.8 0.8 collective-permute-done.8
  270.9 1.1 slice_multiply_fusion.4
  272.5 1.0 broadcast_in_dim.64
  273.6 14.6 %all-to-all-start.1 = ((f32[256,8,128]{2,1,0:T(8,128)}), f32[256,8,128]{2,1,0:T(8,128)}, u32[]{:S(2)}, u32[]{:S(2)}) async-start(f32[256,8,128]{2,1,0:T(8,128)} %broadcast_in_dim.64), calls=%async_computation.1 | async-start | bytes 2097152 | tf_op jit(solution)/shard_map/all_to_all | solution.py:228
  288.2 1.6 squeeze.33
  289.8 28.1 %all-to-all-done.1 = f32[256,8,128]{2,1,0:T(8,128)} async-done(((f32[256,8,128]{2,1,0:T(8,128)}), f32[256,8,128]{2,1,0:T(8,128)}, u32[]{:S(2)}, u32[]{:S(2)}) %all-to-all-start.1) | async-done | bytes 1048608 | tf_op jit(solution)/shard_map/all_to_all | solution.py:228
  317.9 1.4 copy.103
  320.0 1.3 reduce_sum.99
  322.2 1.4 fusion.55
  323.6 1.3 reshape.184
  325.0 1.3 reduce_sum.98
  326.3 2.2 convolution_multiply_fusion
  328.6 1.2 multiply_divide_fusion
  330.8 1.5 fusion.254
  332.2 1.0 broadcast_in_dim.67
  333.2 1.4 reshape.185
  336.4 1.2 slice_multiply_fusion.6
  337.6 1.2 fusion.138
  339.5 0.8 fusion.119
  (127 shorter events, 8.4 us)
Async XLA Ops:
  0.6 6.1 %copy-start.7 = (f32[1,1,32,8,4,128]{5,4,3,2,1,0:T(4,128)S(1)}, f32[1,1,32,8,4,128]{5,4,3,2,1,0:T(4,128)}, u32[]{:S(2)}) copy-start(f32[1,1,32,8,4,128]{5,4,3,2,1,0:T(4,128)} %param.7) | copy-start | bytes 1572868
  12.6 114.1 %all-to-all-start = ((f32[256,4,8,128]{3,2,1,0:T(8,128)}), f32[256,4,8,128]{3,2,1,0:T(8,128)}, u32[]{:S(2)}, u32[]{:S(2)}) async-start(f32[256,4,8,128]{3,2,1,0:T(8,128)} %pad_maximum_fusion), calls=%async_computation | async-start | bytes 8388608 | tf_op jit(solution)/shard_map/all_to_all | solution.py:262
  29.7 1.3 copy-start.11
  30.2 0.8 copy-start.13
  30.2 0.8 copy-start.15
  206.1 18.5 %slice-start = ((f32[4,2,8,2,8,16,8]{5,4,2,6,0,3,1:T(8,128)}), f32[1,2,8,2,8,16,8]{5,4,2,6,0,3,1:T(8,128)S(1)}, s32[]{:S(2)}) async-start(f32[4,2,8,2,8,16,8]{5,4,2,6,0,3,1:T(8,128)} %convolution_bitcast_fusion), calls=%async_computation.2 | async-start | bytes 2097152 | tf_op jit(solution)/shard_map/slice | solution.py:265
  212.5 8.4 %copy-start = (f32[4,16,16,128]{3,2,1,0:T(8,128)}, f32[4,16,16,128]{3,2,1,0:T(8,128)S(1)}, u32[]{:S(2)}) copy-start(f32[4,16,16,128]{3,2,1,0:T(8,128)S(1)} %reshape.178) | copy-start | bytes 1572868
  214.8 12.4 %collective-permute-start.7 = (f32[4,4,4,128]{3,2,1,0:T(4,128)}, f32[4,4,4,128]{3,2,1,0:T(4,128)S(1)}, u32[]{:S(2)}, u32[]{:S(2)}) collective-permute-start(f32[4,4,4,128]{3,2,1,0:T(4,128)} %get-tuple-element.15), channel_id=1, source_target_pairs={{9,0},{10,1},{11,2},{12,3},{13,4},{14,5},{15,6},{17,8},{18,9},{19,... | collective-permute-start | bytes 98312 | tf_op jit(solution)/shard_map/ppermute | solution.py:45
  216.1 26.8 %collective-permute-start.6 = (f32[4,4,16,128]{3,2,1,0:T(8,128)}, f32[4,4,16,128]{3,2,1,0:T(8,128)}, u32[]{:S(2)}, u32[]{:S(2)}) collective-permute-start(f32[4,4,16,128]{3,2,1,0:T(8,128)} %get-tuple-element.19), channel_id=1, source_target_pairs={{8,0},{9,1},{10,2},{11,3},{12,4},{13,5},{14,6},{15,7},{16,8},{17,9... | collective-permute-start | bytes 393224 | tf_op jit(solution)/shard_map/ppermute | solution.py:45
  217.4 15.0 %collective-permute-start.5 = (f32[4,4,4,128]{3,2,1,0:T(4,128)}, f32[4,4,4,128]{3,2,1,0:T(4,128)S(1)}, u32[]{:S(2)}, u32[]{:S(2)}) collective-permute-start(f32[4,4,4,128]{3,2,1,0:T(4,128)} %get-tuple-element.16), channel_id=1, source_target_pairs={{8,1},{9,2},{10,3},{11,4},{12,5},{13,6},{14,7},{16,9},{17,10},{18,... | collective-permute-start | bytes 98312 | tf_op jit(solution)/shard_map/ppermute | solution.py:45
  218.7 24.2 %collective-permute-start.4 = (f32[4,16,4,128]{3,2,1,0:T(4,128)}, f32[4,16,4,128]{3,2,1,0:T(4,128)}, u32[]{:S(2)}, u32[]{:S(2)}) collective-permute-start(f32[4,16,4,128]{3,2,1,0:T(4,128)} %get-tuple-element.21), channel_id=1, source_target_pairs={{1,0},{2,1},{3,2},{4,3},{5,4},{6,5},{7,6},{9,8},{10,9},{11,10},{12... | collective-permute-start | bytes 393224 | tf_op jit(solution)/shard_map/ppermute | solution.py:45
  221.0 21.9 %collective-permute-start.3 = (f32[4,16,4,128]{3,2,1,0:T(4,128)}, f32[4,16,4,128]{3,2,1,0:T(4,128)}, u32[]{:S(2)}, u32[]{:S(2)}) collective-permute-start(f32[4,16,4,128]{3,2,1,0:T(4,128)} %get-tuple-element.20), channel_id=1, source_target_pairs={{0,1},{1,2},{2,3},{3,4},{4,5},{5,6},{6,7},{8,9},{9,10},{10,11},{11... | collective-permute-start | bytes 393224 | tf_op jit(solution)/shard_map/ppermute | solution.py:45
  227.2 9.1 %collective-permute-start.2 = (f32[4,4,4,128]{3,2,1,0:T(4,128)}, f32[4,4,4,128]{3,2,1,0:T(4,128)S(1)}, u32[]{:S(2)}, u32[]{:S(2)}) collective-permute-start(f32[4,4,4,128]{3,2,1,0:T(4,128)} %get-tuple-element.17), channel_id=1, source_target_pairs={{1,8},{2,9},{3,10},{4,11},{5,12},{6,13},{7,14},{9,16},{10,17},{11,... | collective-permute-start | bytes 98312 | tf_op jit(solution)/shard_map/ppermute | solution.py:45
  232.3 10.5 %collective-permute-start.1 = (f32[4,4,16,128]{3,2,1,0:T(8,128)}, f32[4,4,16,128]{3,2,1,0:T(8,128)S(1)}, u32[]{:S(2)}, u32[]{:S(2)}) collective-permute-start(f32[4,4,16,128]{3,2,1,0:T(8,128)} %get-tuple-element.18), channel_id=1, source_target_pairs={{0,8},{1,9},{2,10},{3,11},{4,12},{5,13},{6,14},{7,15},{8,16},{9,17... | collective-permute-start | bytes 393224 | tf_op jit(solution)/shard_map/ppermute | solution.py:45
  236.2 6.6 %collective-permute-start = (f32[4,4,4,128]{3,2,1,0:T(4,128)S(1)}, f32[4,4,4,128]{3,2,1,0:T(4,128)S(1)}, u32[]{:S(2)}, u32[]{:S(2)}) collective-permute-start(f32[4,4,4,128]{3,2,1,0:T(4,128)S(1)} %get-tuple-element.14), channel_id=1, source_target_pairs={{0,9},{1,10},{2,11},{3,12},{4,13},{5,14},{6,15},{8,17},{9,18},{10,... | collective-permute-start | bytes 98312 | tf_op jit(solution)/shard_map/ppermute | solution.py:45
  244.3 1.3 copy-start.9
  244.3 1.3 copy-start.10
  244.4 26.3 %copy-start.12 = (pred[16]{0:T(512)(128)(4,1)S(1)}, pred[16]{0:T(512)(128)(4,1)}, u32[]{:S(2)}) copy-start(pred[16]{0:T(512)(128)(4,1)} %copy-done.11) | copy-start | bytes 52
  244.4 26.3 %copy-start.14 = (pred[16]{0:T(512)(128)(4,1)S(1)}, pred[16]{0:T(512)(128)(4,1)}, u32[]{:S(2)}) copy-start(pred[16]{0:T(512)(128)(4,1)} %copy-done.13) | copy-start | bytes 52
  244.4 26.3 %copy-start.16 = (pred[16]{0:T(512)(128)(4,1)S(1)}, pred[16]{0:T(512)(128)(4,1)}, u32[]{:S(2)}) copy-start(pred[16]{0:T(512)(128)(4,1)} %copy-done.15) | copy-start | bytes 52
  244.7 0.7 copy-start.1
  246.0 10.1 %collective-permute-start.15 = (f32[2,4,4,64]{3,2,1,0:T(4,128)S(1)}, f32[2,4,4,64]{3,2,1,0:T(4,128)S(1)}, u32[]{:S(2)}, u32[]{:S(2)}) collective-permute-start(f32[2,4,4,64]{3,2,1,0:T(4,128)S(1)} %get-tuple-element.33), channel_id=1, source_target_pairs={{9,0},{10,1},{11,2},{12,3},{13,4},{14,5},{15,6},{17,8},{18,9},{19,... | collective-permute-start | bytes 24584 | tf_op jit(solution)/shard_map/ppermute | solution.py:45
  247.3 12.5 %collective-permute-start.13 = (f32[2,4,4,64]{3,2,1,0:T(4,128)S(1)}, f32[2,4,4,64]{3,2,1,0:T(4,128)S(1)}, u32[]{:S(2)}, u32[]{:S(2)}) collective-permute-start(f32[2,4,4,64]{3,2,1,0:T(4,128)S(1)} %get-tuple-element.32), channel_id=1, source_target_pairs={{8,1},{9,2},{10,3},{11,4},{12,5},{13,6},{14,7},{16,9},{17,10},{18,... | collective-permute-start | bytes 24584 | tf_op jit(solution)/shard_map/ppermute | solution.py:45
  248.6 17.0 %collective-permute-start.10 = (f32[2,4,4,64]{3,2,1,0:T(4,128)S(1)}, f32[2,4,4,64]{3,2,1,0:T(4,128)S(1)}, u32[]{:S(2)}, u32[]{:S(2)}) collective-permute-start(f32[2,4,4,64]{3,2,1,0:T(4,128)S(1)} %get-tuple-element.31), channel_id=1, source_target_pairs={{1,8},{2,9},{3,10},{4,11},{5,12},{6,13},{7,14},{9,16},{10,17},{11,... | collective-permute-start | bytes 24584 | tf_op jit(solution)/shard_map/ppermute | solution.py:45
  252.9 17.7 %collective-permute-start.14 = (f32[2,4,8,64]{3,2,1,0:T(8,128)S(1)}, f32[2,4,8,64]{3,2,1,0:T(8,128)S(1)}, u32[]{:S(2)}, u32[]{:S(2)}) collective-permute-start(f32[2,4,8,64]{3,2,1,0:T(8,128)S(1)} %get-tuple-element.35), channel_id=1, source_target_pairs={{8,0},{9,1},{10,2},{11,3},{12,4},{13,5},{14,6},{15,7},{16,8},{17,9... | collective-permute-start | bytes 49160 | tf_op jit(solution)/shard_map/ppermute | solution.py:45
  254.2 16.5 %collective-permute-start.12 = (f32[2,8,4,64]{3,2,1,0:T(4,128)S(1)}, f32[2,8,4,64]{3,2,1,0:T(4,128)S(1)}, u32[]{:S(2)}, u32[]{:S(2)}) collective-permute-start(f32[2,8,4,64]{3,2,1,0:T(4,128)S(1)} %get-tuple-element.37), channel_id=1, source_target_pairs={{1,0},{2,1},{3,2},{4,3},{5,4},{6,5},{7,6},{9,8},{10,9},{11,10},{12... | collective-permute-start | bytes 49160 | tf_op jit(solution)/shard_map/ppermute | solution.py:45
  256.1 14.5 %collective-permute-start.11 = (f32[2,8,4,64]{3,2,1,0:T(4,128)S(1)}, f32[2,8,4,64]{3,2,1,0:T(4,128)S(1)}, u32[]{:S(2)}, u32[]{:S(2)}) collective-permute-start(f32[2,8,4,64]{3,2,1,0:T(4,128)S(1)} %get-tuple-element.36), channel_id=1, source_target_pairs={{0,1},{1,2},{2,3},{3,4},{4,5},{5,6},{6,7},{8,9},{9,10},{10,11},{11... | collective-permute-start | bytes 49160 | tf_op jit(solution)/shard_map/ppermute | solution.py:45
  259.8 10.9 %collective-permute-start.9 = (f32[2,4,8,64]{3,2,1,0:T(8,128)S(1)}, f32[2,4,8,64]{3,2,1,0:T(8,128)S(1)}, u32[]{:S(2)}, u32[]{:S(2)}) collective-permute-start(f32[2,4,8,64]{3,2,1,0:T(8,128)S(1)} %get-tuple-element.34), channel_id=1, source_target_pairs={{0,8},{1,9},{2,10},{3,11},{4,12},{5,13},{6,14},{7,15},{8,16},{9,17... | collective-permute-start | bytes 49160 | tf_op jit(solution)/shard_map/ppermute | solution.py:45
  265.6 5.0 %collective-permute-start.8 = (f32[2,4,4,64]{3,2,1,0:T(4,128)S(1)}, f32[2,4,4,64]{3,2,1,0:T(4,128)S(1)}, u32[]{:S(2)}, u32[]{:S(2)}) collective-permute-start(f32[2,4,4,64]{3,2,1,0:T(4,128)S(1)} %get-tuple-element.30), channel_id=1, source_target_pairs={{0,9},{1,10},{2,11},{3,12},{4,13},{5,14},{6,15},{8,17},{9,18},{10,... | collective-permute-start | bytes 24584 | tf_op jit(solution)/shard_map/ppermute | solution.py:45
  270.8 1.4 copy-start.6
  270.9 1.2 copy-start.3
  270.9 1.3 copy-start.5
  273.6 44.4 %all-to-all-start.1 = ((f32[256,8,128]{2,1,0:T(8,128)}), f32[256,8,128]{2,1,0:T(8,128)}, u32[]{:S(2)}, u32[]{:S(2)}) async-start(f32[256,8,128]{2,1,0:T(8,128)} %broadcast_in_dim.64), calls=%async_computation.1 | async-start | bytes 2097152 | tf_op jit(solution)/shard_map/all_to_all | solution.py:228
  326.3 2.3 copy-start.8
  334.7 2.9 copy-start.4
  335.3 3.9 %copy-start.2 = (f32[22,22,128]{2,1,0:T(8,128)S(1)}, f32[22,22,128]{2,1,0:T(8,128)}, u32[]{:S(2)}) copy-start(f32[22,22,128]{2,1,0:T(8,128)} %copy-done.1) | copy-start | bytes 743428
